TPU v7x, 128 devices: a whole 4x4x4 slice. The times are simulated.
128 devices in a mesh: lon: 8 (over x, core), lat: 16 (over y, z).
Axes of the slice: x: 4, y: 4, z: 4, core: 2. Of those that a mesh axis runs over, the one named last changes fastest.
Arguments:
- owner_tile: int32 [262144], P(('lon', 'lat')), may hold values from 0 to 127, as said below
- corner_cell: int32 [262144], P(('lon', 'lat')), may hold values from 0 to 36448
- weights: bfloat16 [4, 262144], P(None, ('lon', 'lat')), may hold values from 0.19921875 to 1
- innovations: bfloat16 [16, 262144], P(None, ('lon', 'lat')), may hold values from -6 to 6
- x_inverse: bfloat16 [2304, 2304], replicated, may hold values from 0 to 2
- y_inverse: bfloat16 [2048, 2048], replicated, may hold values from 0 to 2
Outputs:
- analysis_increment: bfloat16 [16, 2304, 2048], P(None, 'lon', 'lat')
Inputs may be any that keep to these rules, and one draw needn't show every extreme that they name: `owner_tile`: among the observations of one device no tile appears more than 40 times; in every draw all 8 tiles of one latitude row appear exactly 40 times among the observations of every device.
All inputs are finite; a program needn't handle non-finite values.
Results may differ from a plain program's by a relative error of at most 0.0054.
Values may be sent and summed in bfloat16 or wider, within the bound.
No kernel may reach another device: no remote copies, remote signals or barrier semaphores. Data moves between devices by JAX's collectives and lax.ppermute only.
A program may use at most 192 MiB of HBM per device.

v0:
```python
import jax
import jax.numpy as jnp
from jax import lax
from jax.sharding import PartitionSpec as P


def tile_ranks(owner_tile, groups):
    obs_total = owner_tile.shape[0]
    block = 128
    blocks = obs_total // block
    one_hot = (owner_tile[:, None] == jnp.arange(groups, dtype=jnp.int32)[None, :]).astype(
        jnp.bfloat16
    )
    hot_blocks = one_hot.reshape(blocks, block, groups)
    inner = jnp.arange(block, dtype=jnp.int32)
    lower = (inner[None, :] <= inner[:, None]).astype(jnp.bfloat16)
    within = jnp.einsum("ij,bjd->bid", lower, hot_blocks, preferred_element_type=jnp.float32)
    totals = jnp.sum(hot_blocks.astype(jnp.float32), axis=1).astype(jnp.bfloat16)
    outer = jnp.arange(blocks, dtype=jnp.int32)
    before = (outer[None, :] < outer[:, None]).astype(jnp.bfloat16)
    earlier = jnp.dot(before, totals, preferred_element_type=jnp.float32)
    running = (within + earlier[:, None, :]).reshape(obs_total, groups)
    rank = jnp.sum(running * one_hot.astype(jnp.float32), axis=1).astype(jnp.int32) - 1
    return one_hot, rank


def route_obs(owner_tile, corner_cell, weights, innovations, groups, capacity, tile_cols):
    one_hot, rank = tile_ranks(owner_tile, groups)
    cell_x = corner_cell // (tile_cols - 1)
    cell_y = corner_cell % (tile_cols - 1)
    digits = jnp.stack([cell_y, cell_x % 128, cell_x // 128]).astype(jnp.bfloat16)
    stacked = jnp.concatenate([innovations, weights, digits], 0)
    rows = stacked.shape[0]
    rank_hot = rank[None, :] == jnp.arange(capacity, dtype=jnp.int32)[:, None]
    spread = jnp.where(rank_hot[None, :, :], stacked[:, None, :], jnp.zeros((), jnp.bfloat16))
    spread = spread.reshape(rows * capacity, -1)
    send = lax.dot_general(
        one_hot, spread, (((0,), (1,)), ((), ())), preferred_element_type=jnp.float32
    ).astype(jnp.bfloat16)
    lat_count = lax.axis_size("lat")
    send = send.reshape(groups // lat_count, lat_count, rows * capacity)
    hop = lax.all_to_all(send, "lat", 1, 1, tiled=True)
    got = lax.all_to_all(hop, "lon", 0, 0, tiled=True)
    got = got.reshape(groups, rows, capacity).transpose(1, 0, 2).reshape(rows, -1)
    return got


def deposit(got, channels, tile_rows, tile_cols):
    values = got[:channels]
    got_weights = got[channels : channels + 4]
    base_y = got[channels + 4].astype(jnp.int32)
    base_x = got[channels + 5].astype(jnp.int32) + 128 * got[channels + 6].astype(jnp.int32)
    row_iota = jnp.arange(tile_rows, dtype=jnp.int32)
    col_iota = jnp.arange(tile_cols, dtype=jnp.int32)
    zero_value = jnp.zeros((), jnp.bfloat16)
    raw_total = jnp.zeros((channels, tile_rows, tile_cols), jnp.float32)
    for offset_y in range(2):
        near_rows = jnp.where(
            row_iota[None, :] == base_x[:, None], got_weights[2 * offset_y][:, None], zero_value
        )
        near_rows = near_rows + jnp.where(
            row_iota[None, :] == base_x[:, None] + 1,
            got_weights[2 * offset_y + 1][:, None],
            zero_value,
        )
        spread = jnp.where(
            col_iota[None, :, None] == (base_y + offset_y)[None, None, :],
            values[:, None, :],
            zero_value,
        )
        raw_total = raw_total + jnp.einsum(
            "cyo,ox->cxy", spread, near_rows, preferred_element_type=jnp.float32
        )
    return raw_total.astype(jnp.bfloat16)


def shards(owner_tile, corner_cell, weights, innovations, x_inverse, y_inverse):
    lon_count = lax.axis_size("lon")
    lat_count = lax.axis_size("lat")
    devices = lon_count * lat_count
    channels = innovations.shape[0]
    obs_count = innovations.shape[1]
    line_x = x_inverse.shape[0]
    tile_rows = line_x // lon_count
    line_y = y_inverse.shape[0]
    tile_cols = line_y // lat_count
    capacity = 5 * obs_count // (2 * devices)
    got = route_obs(owner_tile, corner_cell, weights, innovations, devices, capacity, tile_cols)
    increment = deposit(got, channels, tile_rows, tile_cols)
    pair = channels // lon_count
    lanes = pair * tile_cols
    by_pair = increment.reshape(lon_count, pair, tile_rows, tile_cols).transpose(0, 2, 1, 3)
    by_pair = by_pair.reshape(lon_count, tile_rows, lanes)
    lines_x = lax.all_to_all(by_pair, "lon", 0, 0, tiled=True).reshape(line_x, lanes)
    solved_x = jnp.dot(x_inverse, lines_x, preferred_element_type=jnp.float32).astype(jnp.bfloat16)
    back_x = lax.all_to_all(solved_x, "lon", 0, 1, tiled=True)
    lines_y = lax.all_to_all(back_x, "lat", 1, 1, tiled=True)
    solved_y = lax.dot_general(
        lines_y, y_inverse, (((1,), (1,)), ((), ())), preferred_element_type=jnp.float32
    ).astype(jnp.bfloat16)
    solved_y = solved_y.reshape(tile_rows, lat_count, tile_cols)
    tiles = lax.all_to_all(solved_y, "lat", 1, 1, tiled=True)
    return tiles.transpose(1, 0, 2)


def solution(mesh):
    placed = (
        P(("lon", "lat")),
        P(("lon", "lat")),
        P(None, ("lon", "lat")),
        P(None, ("lon", "lat")),
        P(),
        P(),
    )
    return jax.shard_map(
        shards, mesh=mesh, in_specs=placed, out_specs=P(None, "lon", "lat"), check_vma=False
    )
```

profile of v0, /device:TPU:0, one launch (start us, length us, event | category | flops | bytes accessed | tf_op | source)
XLA Modules:
  0.0 155.7 jit_solution(13154653239799445792)
XLA Ops:
  0.0 0.0 copy-start
  0.0 1.0 fusion.44
  1.0 0.1 fusion.56
  1.1 1.2 fusion.40
  2.3 0.7 fusion.55
  3.2 1.6 %concatenate.4 = bf16[23,2048]{1,0:T(8,128)(2,1)S(1)} concatenate(bf16[16,2048]{1,0:T(8,128)(2,1)} %param.9, bf16[4,2048]{1,0:T(4,128)(2,1)} %param.8, bf16[1,2048]{1,0:T(2,128)(2,1)S(1)} %stack.14, bf16[1,2048]{1,0:T(2,128)(2,1)S(1)} %stack.15, bf16[1,2048]{1,0:T(2,128)(2,1)S(1)} %stack.16), dimensions={0} | concatenate | bytes 188416 | tf_op jit(solution)/shard_map/concatenate | solution.py:32
  4.8 0.4 broadcast_select_fusion
  5.1 0.0 copy-done
  5.2 1.3 convolution_convert_fusion.2
  6.4 0.2 copy.34
  6.6 0.2 copy.35
  6.7 16.5 %all_to_all.48 = bf16[8,16,920]{2,0,1:T(8,128)(2,1)S(1)} all-to-all(bf16[8,16,920]{2,0,1:T(8,128)(2,1)S(1)} %copy.35), channel_id=1, replica_groups=mesh['lon'=8,'lat'=16] {'lat'}, dimensions={1} | all-to-all | bytes 471040 | tf_op jit(solution)/shard_map/all_to_all | solution.py:42
  23.2 0.1 copy.36
  23.4 11.6 %all_to_all.49 = bf16[8,16,920]{2,1,0:T(8,128)(2,1)S(1)} all-to-all(bf16[8,16,920]{2,1,0:T(8,128)(2,1)S(1)} %copy.36), channel_id=1, replica_groups=mesh['lon'=8,'lat'=16] {'lon'}, dimensions={0} | all-to-all | bytes 471040 | tf_op jit(solution)/shard_map/all_to_all | solution.py:43
  35.0 0.7 reshape.194
  35.7 0.8 slice_reduce_fusion.3
  36.5 0.6 fusion.50
  37.1 0.1 reshape.199
  37.2 0.3 iota_compare_fusion.3
  37.5 0.1 broadcast_in_dim.117
  37.7 0.1 broadcast_in_dim.126
  37.8 0.1 broadcast_in_dim.120
  37.9 0.1 broadcast_in_dim.128
  38.0 0.1 copy.37
  38.1 0.7 broadcast_in_dim.123
  38.9 0.1 add.75
  39.0 0.3 iota_compare_fusion.2
  39.3 7.9 %fusion = f32[288,16,128]{2,0,1:T(8,128)} fusion(pred[128,5120]{1,0:T(8,128)(4,1)S(1)} %iota_compare_fusion.2, bf16[16,5120]{1,0:T(8,128)(2,1)S(1)} %broadcast_in_dim.123, s32[5120]{0:T(1024)S(1)} %broadcast_add_fusion.1, s32[5120]{0:T(1024)S(1)} %add.75, bf16[5120]{0:T(1024)(128)(2,1)S(1)} %broadcast_in_dim.128, bf16[5120]{0:T(1024)(128)(2,1)S(1)} %broadcast_in_dim.126), kind=kOutput, calls=%fused_computation | convolution fusion | flops 6062080000 | bytes 3239936 | tf_op jit(solution)/shard_map/cyo,ox->cxy/dot_general | solution.py:71
  47.3 8.2 %add_convert_fusion = bf16[288,16,128]{2,0,1:T(8,128)(2,1)S(1)} fusion(f32[288,16,128]{2,0,1:T(8,128)} %fusion, pred[128,5120]{1,0:T(8,128)(4,1)S(1)} %iota_compare_fusion.3, bf16[16,5120]{1,0:T(8,128)(2,1)S(1)} %broadcast_in_dim.123, s32[5120]{0:T(1024)S(1)} %broadcast_add_fusion.1, s32[5120]{0:T(1024)S(1)} %add.75, ...), kind=kOutput, calls=%fused_computation.30 | convolution fusion | flops 6063259648 | bytes 4419584 | tf_op jit(solution)/shard_map/cyo,ox->cxy/dot_general | solution.py:71
  55.5 1.0 copy.53
  56.5 1.0 reshape.196
  57.5 19.8 %all_to_all.50 = bf16[8,288,256]{2,1,0:T(8,128)(2,1)S(1)} all-to-all(bf16[8,288,256]{2,1,0:T(8,128)(2,1)S(1)} %reshape.196), channel_id=1, replica_groups=mesh['lon'=8,'lat'=16] {'lon'}, dimensions={0} | all-to-all | bytes 2359296 | tf_op jit(solution)/shard_map/all_to_all | solution.py:94
  77.3 7.1 %fusion.14 = bf16[2304,256]{0,1:T(8,128)(2,1)S(1)} fusion(bf16[2304,256]{1,0:T(8,128)(2,1)S(1)} %bitcast.62, bf16[2304,2304]{1,0:T(8,128)(2,1)} %param.10), kind=kOutput, calls=%fused_computation.18 | convolution fusion | flops 2718498816 | bytes 12976128 | tf_op jit(solution)/shard_map/dot_general | solution.py:95
  84.4 0.6 copy.39
  85.0 19.8 %all_to_all.51 = bf16[8,288,256]{2,1,0:T(8,128)(2,1)S(1)} all-to-all(bf16[8,288,256]{2,1,0:T(8,128)(2,1)S(1)} %bitcast.54), channel_id=1, replica_groups=mesh['lon'=8,'lat'=16] {'lon'}, dimensions={0} | all-to-all | bytes 2359296 | tf_op jit(solution)/shard_map/all_to_all | solution.py:96
  104.8 0.7 copy.40
  105.5 0.4 all_to_all.38
  105.9 0.3 copy.41
  106.2 21.6 %all_to_all.52 = bf16[288,16,128]{2,0,1:T(8,128)(2,1)S(1)} all-to-all(bf16[288,16,128]{2,0,1:T(8,128)(2,1)S(1)} %copy.41), channel_id=1, replica_groups=mesh['lon'=8,'lat'=16] {'lat'}, dimensions={1} | all-to-all | bytes 2359296 | tf_op jit(solution)/shard_map/all_to_all | solution.py:97
  127.8 6.0 %fusion.37 = bf16[36,16,8,128]{3,2,1,0:T(8,128)(2,1)S(1)} fusion(bf16[2048,2048]{1,0:T(8,128)(2,1)} %param.11, bf16[288,16,128]{2,0,1:T(8,128)(2,1)S(1)} %all_to_all.52), kind=kOutput, calls=%fused_computation.37 | convolution fusion | flops 2416508928 | bytes 10747904 | tf_op jit(solution)/shard_map/dot_general | solution.py:98
  133.8 0.2 copy.52
  134.0 20.6 %all_to_all.53 = bf16[288,16,128]{2,0,1:T(8,128)(2,1)S(1)} all-to-all(bf16[288,16,128]{2,0,1:T(8,128)(2,1)S(1)} %bitcast.56), channel_id=1, replica_groups=mesh['lon'=8,'lat'=16] {'lat'}, dimensions={1} | all-to-all | bytes 2359296 | tf_op jit(solution)/shard_map/all_to_all | solution.py:102
  154.6 1.0 copy.55
  (8 shorter events, 0.1 us)
Async XLA Ops:
  0.0 5.1 %copy-start = (s32[2048]{0:T(1024)S(1)}, s32[2048]{0:T(1024)}, u32[]{:S(2)}) copy-start(s32[2048]{0:T(1024)} %param.6) | copy-start | bytes 24580
where the time goes:
time: 156 us
  blocking collectives  110 us (71%)
  matrix products  31.8 us (20%)
  local copies, waits for them, and re-layouts  10.4 us (7%)
  other arithmetic  3.39 us (2%)
    all_to_all x1, blocking collectives, shards(): lines_y = lax.all_to_all(back_x, 'lat', 1, 1, tiled=True)  21.6 us
    all_to_all x1, blocking collectives, shards(): tiles = lax.all_to_all(solved_y, 'lat', 1, 1, tiled=True)  20.6 us
    all_to_all x1, blocking collectives, shards(): lax.all_to_all(by_pair, 'lon', 0, 0, tiled=True).reshape(line_x, lanes)  19.8 us
    all_to_all x1, blocking collectives, shards(): back_x = lax.all_to_all(solved_x, 'lon', 0, 1, tiled=True)  19.8 us
    all_to_all x1, blocking collectives, route_obs(): hop = lax.all_to_all(send, 'lat', 1, 1, tiled=True)  16.5 us
    dot_general x2, matrix products, deposit(): jnp.einsum('cyo,ox->cxy', spread, near_rows, preferred_element_type=jnp.f...  16.2 us
    all_to_all x1, blocking collectives, route_obs(): got = lax.all_to_all(hop, 'lon', 0, 0, tiled=True)  11.6 us
    dot_general x1, matrix products, shards(): jnp.dot(x_inverse, lines_x, preferred_element_type=jnp.float32)  7.06 us

commit v1 on v0

--- a/solution.py
+++ b/solution.py
@@ -37,10 +37,7 @@
     send = lax.dot_general(
         one_hot, spread, (((0,), (1,)), ((), ())), preferred_element_type=jnp.float32
     ).astype(jnp.bfloat16)
-    lat_count = lax.axis_size("lat")
-    send = send.reshape(groups // lat_count, lat_count, rows * capacity)
-    hop = lax.all_to_all(send, "lat", 1, 1, tiled=True)
-    got = lax.all_to_all(hop, "lon", 0, 0, tiled=True)
+    got = lax.all_to_all(send, ("lon", "lat"), 0, 0, tiled=True)
     got = got.reshape(groups, rows, capacity).transpose(1, 0, 2).reshape(rows, -1)
     return got
 
@@ -93,14 +90,18 @@
     by_pair = by_pair.reshape(lon_count, tile_rows, lanes)
     lines_x = lax.all_to_all(by_pair, "lon", 0, 0, tiled=True).reshape(line_x, lanes)
     solved_x = jnp.dot(x_inverse, lines_x, preferred_element_type=jnp.float32).astype(jnp.bfloat16)
-    back_x = lax.all_to_all(solved_x, "lon", 0, 1, tiled=True)
-    lines_y = lax.all_to_all(back_x, "lat", 1, 1, tiled=True)
+    stride = tile_rows // lat_count
+    by_row = solved_x.reshape(lon_count, stride, lat_count, lanes).transpose(0, 2, 1, 3)
+    by_row = by_row.reshape(devices, stride, lanes)
+    got = lax.all_to_all(by_row, ("lon", "lat"), 0, 0, tiled=True)
+    got = got.reshape(lon_count, lat_count, stride, pair, tile_cols).transpose(0, 3, 2, 1, 4)
+    lines_y = got.reshape(channels * stride, line_y)
     solved_y = lax.dot_general(
         lines_y, y_inverse, (((1,), (1,)), ((), ())), preferred_element_type=jnp.float32
     ).astype(jnp.bfloat16)
-    solved_y = solved_y.reshape(tile_rows, lat_count, tile_cols)
+    solved_y = solved_y.reshape(channels * stride, lat_count, tile_cols)
     tiles = lax.all_to_all(solved_y, "lat", 1, 1, tiled=True)
-    return tiles.transpose(1, 0, 2)
+    return tiles.reshape(channels, tile_rows, tile_cols)
 
 
 def solution(mesh):

time: 156 us -> 139 us (0.89)
  blocking collectives: 110 us -> 91.3 us
    all_to_all x4 -> x2, blocking collectives: 69.5 us -> 50.5 us  [the longest x1 28.7 us: shards(): got = lax.all_to_all(by_row, ('lon', 'lat'), 0, 0, tiled=True)]
where the time goes in v1:
time: 139 us
  blocking collectives  91.3 us (66%)
  matrix products  31.8 us (23%)
  local copies, waits for them, and re-layouts  11.7 us (8%)
  other arithmetic  3.65 us (3%)
    all_to_all x1, blocking collectives, shards(): got = lax.all_to_all(by_row, ('lon', 'lat'), 0, 0, tiled=True)  28.7 us
    all_to_all x1, blocking collectives, route_obs(): got = lax.all_to_all(send, ('lon', 'lat'), 0, 0, tiled=True)  21.8 us
    all_to_all x1, blocking collectives, shards(): tiles = lax.all_to_all(solved_y, 'lat', 1, 1, tiled=True)  21 us
    all_to_all x1, blocking collectives, shards(): lax.all_to_all(by_pair, 'lon', 0, 0, tiled=True).reshape(line_x, lanes)  19.8 us
    dot_general x2, matrix products, deposit(): jnp.einsum('cyo,ox->cxy', spread, near_rows, preferred_element_type=jnp.f...  16.2 us
    dot_general x1, matrix products, shards(): jnp.dot(x_inverse, lines_x, preferred_element_type=jnp.float32)  7.06 us
    dot_general x1, matrix products, shards(): lax.dot_general(lines_y, y_inverse, (((1,), (1,)), ((), ())), preferred_e...  6.02 us

profile of v1, /device:TPU:0, one launch (start us, length us, event | category | flops | bytes accessed | tf_op | source)
XLA Modules:
  0.0 138.7 jit_solution(12283854841983395752)
XLA Ops:
  0.0 0.0 copy-start
  0.0 1.0 fusion.45
  1.0 0.1 fusion.53
  1.1 1.2 fusion.40
  2.3 0.7 fusion.52
  3.2 1.6 %concatenate.4 = bf16[23,2048]{1,0:T(8,128)(2,1)S(1)} concatenate(bf16[16,2048]{1,0:T(8,128)(2,1)} %param.9, bf16[4,2048]{1,0:T(4,128)(2,1)} %param.8, bf16[1,2048]{1,0:T(2,128)(2,1)S(1)} %stack.14, bf16[1,2048]{1,0:T(2,128)(2,1)S(1)} %stack.15, bf16[1,2048]{1,0:T(2,128)(2,1)S(1)} %stack.16), dimensions={0} | concatenate | bytes 188416 | tf_op jit(solution)/shard_map/concatenate | solution.py:32
  4.8 0.4 broadcast_select_fusion
  5.1 0.0 copy-done
  5.2 1.3 fusion.43
  6.4 0.5 broadcast.125
  6.9 0.8 reduce.2
  7.7 0.2 copy.50
  7.9 0.3 reshape.217
  8.2 21.8 %all_to_all.24 = bf16[128,2,460]{2,1,0:T(2,128)(2,1)S(1)} all-to-all(bf16[128,2,460]{2,1,0:T(2,128)(2,1)S(1)} %reshape.217), channel_id=1, replica_groups=mesh['lon'=8,'lat'=16] {'lon','lat'}, dimensions={0} | all-to-all | bytes 471040 | tf_op jit(solution)/shard_map/all_to_all | solution.py:40
  30.0 0.4 reshape.218
  30.4 0.7 copy.22
  31.2 0.1 copy.26
  31.3 0.1 reshape.212
  31.4 0.3 iota_compare_fusion.3
  31.7 0.1 copy.23
  31.8 0.1 add.75
  32.0 0.1 copy.24
  32.1 0.1 broadcast_in_dim.117
  32.2 0.1 copy.28
  32.3 0.1 broadcast_in_dim.126
  32.4 0.1 copy.25
  32.6 0.1 broadcast_in_dim.120
  32.7 0.1 copy.29
  32.8 0.1 broadcast_in_dim.128
  32.9 0.3 copy.27
  33.2 0.7 broadcast_in_dim.123
  33.9 0.3 iota_compare_fusion.2
  34.3 7.9 %fusion = f32[288,16,128]{2,0,1:T(8,128)} fusion(pred[128,5120]{1,0:T(8,128)(4,1)S(1)} %iota_compare_fusion.2, bf16[16,5120]{1,0:T(8,128)(2,1)S(1)} %broadcast_in_dim.123, s32[5120]{0:T(1024)S(1)} %broadcast_add_fusion.1, s32[5120]{0:T(1024)S(1)} %add.75, bf16[5120]{0:T(1024)(128)(2,1)S(1)} %broadcast_in_dim.128, bf16[5120]{0:T(1024)(128)(2,1)S(1)} %broadcast_in_dim.126), kind=kOutput, calls=%fused_computation | convolution fusion | flops 6062080000 | bytes 3239936 | tf_op jit(solution)/shard_map/cyo,ox->cxy/dot_general | solution.py:68
  42.2 8.2 %add_convert_fusion = bf16[288,16,128]{2,0,1:T(8,128)(2,1)S(1)} fusion(f32[288,16,128]{2,0,1:T(8,128)} %fusion, pred[128,5120]{1,0:T(8,128)(4,1)S(1)} %iota_compare_fusion.3, bf16[16,5120]{1,0:T(8,128)(2,1)S(1)} %broadcast_in_dim.123, s32[5120]{0:T(1024)S(1)} %broadcast_add_fusion.1, s32[5120]{0:T(1024)S(1)} %add.75, ...), kind=kOutput, calls=%fused_computation.30 | convolution fusion | flops 6063259648 | bytes 4419584 | tf_op jit(solution)/shard_map/cyo,ox->cxy/dot_general | solution.py:68
  50.5 1.0 copy.49
  51.5 0.8 reshape.204
  52.3 19.8 %all_to_all.25 = bf16[8,288,256]{2,1,0:T(8,128)(2,1)S(1)} all-to-all(bf16[8,288,256]{2,1,0:T(8,128)(2,1)S(1)} %reshape.204), channel_id=1, replica_groups=mesh['lon'=8,'lat'=16] {'lon'}, dimensions={0} | all-to-all | bytes 2359296 | tf_op jit(solution)/shard_map/all_to_all | solution.py:91
  72.0 7.1 %fusion.14 = bf16[2304,256]{0,1:T(8,128)(2,1)S(1)} fusion(bf16[2304,256]{1,0:T(8,128)(2,1)S(1)} %bitcast.64, bf16[2304,2304]{1,0:T(8,128)(2,1)} %param.10), kind=kOutput, calls=%fused_computation.18 | convolution fusion | flops 2718498816 | bytes 12976128 | tf_op jit(solution)/shard_map/dot_general | solution.py:92
  79.1 0.6 copy.31
  79.7 0.1 copy.32
  79.9 0.7 copy.33
  80.6 28.7 %all_to_all.26 = bf16[128,18,256]{2,1,0:T(8,128)(2,1)S(1)} all-to-all(bf16[128,18,256]{2,1,0:T(8,128)(2,1)S(1)} %copy.33), channel_id=1, replica_groups=mesh['lon'=8,'lat'=16] {'lon','lat'}, dimensions={0} | all-to-all | bytes 2359296 | tf_op jit(solution)/shard_map/all_to_all | solution.py:96
  109.3 0.6 reshape.216
  109.8 0.2 copy.35
  110.0 6.0 %fusion.37 = bf16[36,16,8,128]{3,2,1,0:T(8,128)(2,1)S(1)} fusion(bf16[2048,2048]{1,0:T(8,128)(2,1)} %param.11, bf16[36,8,16,128]{3,2,1,0:T(8,128)(2,1)S(1)} %bitcast.65), kind=kOutput, calls=%fused_computation.37 | convolution fusion | flops 2416508928 | bytes 10747904 | tf_op jit(solution)/shard_map/dot_general | solution.py:99
  116.0 0.2 copy.48
  116.2 21.0 %all_to_all.27 = bf16[288,16,128]{2,0,1:T(8,128)(2,1)S(1)} all-to-all(bf16[288,16,128]{2,0,1:T(8,128)(2,1)S(1)} %bitcast.60), channel_id=1, replica_groups=mesh['lon'=8,'lat'=16] {'lat'}, dimensions={1} | all-to-all | bytes 2359296 | tf_op jit(solution)/shard_map/all_to_all | solution.py:103
  137.2 1.5 %copy.37 = bf16[288,16,128]{2,1,0:T(8,128)(2,1)} copy(bf16[288,16,128]{2,0,1:T(8,128)(2,1)S(1)} %all_to_all.27) | data formatting | bytes 2359296 | tf_op jit(solution)/shard_map/all_to_all | solution.py:103
  (10 shorter events, 0.1 us)
Async XLA Ops:
  0.0 5.1 %copy-start = (s32[2048]{0:T(1024)S(1)}, s32[2048]{0:T(1024)}, u32[]{:S(2)}) copy-start(s32[2048]{0:T(1024)} %param.6) | copy-start | bytes 24580

commit v2 on v1

--- a/solution.py
+++ b/solution.py
@@ -50,7 +50,7 @@
     row_iota = jnp.arange(tile_rows, dtype=jnp.int32)
     col_iota = jnp.arange(tile_cols, dtype=jnp.int32)
     zero_value = jnp.zeros((), jnp.bfloat16)
-    raw_total = jnp.zeros((channels, tile_rows, tile_cols), jnp.float32)
+    near = []
     for offset_y in range(2):
         near_rows = jnp.where(
             row_iota[None, :] == base_x[:, None], got_weights[2 * offset_y][:, None], zero_value
@@ -60,15 +60,14 @@
             got_weights[2 * offset_y + 1][:, None],
             zero_value,
         )
-        spread = jnp.where(
-            col_iota[None, :, None] == (base_y + offset_y)[None, None, :],
-            values[:, None, :],
-            zero_value,
-        )
-        raw_total = raw_total + jnp.einsum(
-            "cyo,ox->cxy", spread, near_rows, preferred_element_type=jnp.float32
-        )
-    return raw_total.astype(jnp.bfloat16)
+        near.append(near_rows)
+    near = jnp.stack(near, 1)
+    spread = jnp.where(
+        col_iota[None, :, None] == base_y[None, None, :], values[:, None, :], zero_value
+    )
+    both = jnp.einsum("cyo,odx->dcxy", spread, near, preferred_element_type=jnp.float32)
+    shifted = jnp.pad(both[1, :, :, :-1], ((0, 0), (0, 0), (1, 0)))
+    return (both[0] + shifted).astype(jnp.bfloat16)
 
 
 def shards(owner_tile, corner_cell, weights, innovations, x_inverse, y_inverse):

time: 139 us -> 147 us (1.058)
  other arithmetic: 3.65 us -> 8.97 us
  local copies, waits for them, and re-layouts: 11.7 us -> 14.7 us
    add x1, other arithmetic: 0.01 us -> 4.16 us  [deposit(): near_rows + jnp.where(row_iota[None, :] == base_x[:, None] + 1, got_weigh...]
    squeeze x0 -> x1, local copies, waits for them, and re-layouts: none -> 1.98 us  [deposit(): shifted = jnp.pad(both[1, :, :, :-1], ((0, 0), (0, 0), (1, 0)))]
    dot_general x2 -> x1, matrix products: 16.2 us -> 15.6 us  [deposit(): jnp.einsum('cyo,odx->dcxy', spread, near, preferred_element_type=jnp.floa...]
where the time goes in v2:
time: 147 us; the launch traced here: 146 us
  blocking collectives  91.3 us (62%)
  matrix products  31.2 us (21%)
  local copies, waits for them, and re-layouts  14.7 us (10%)
  other arithmetic  8.97 us (6%)
    all_to_all x1, blocking collectives, shards(): got = lax.all_to_all(by_row, ('lon', 'lat'), 0, 0, tiled=True)  28.7 us
    all_to_all x1, blocking collectives, route_obs(): got = lax.all_to_all(send, ('lon', 'lat'), 0, 0, tiled=True)  21.8 us
    all_to_all x1, blocking collectives, shards(): tiles = lax.all_to_all(solved_y, 'lat', 1, 1, tiled=True)  21 us
    all_to_all x1, blocking collectives, shards(): lax.all_to_all(by_pair, 'lon', 0, 0, tiled=True).reshape(line_x, lanes)  19.8 us
    dot_general x1, matrix products, deposit(): jnp.einsum('cyo,odx->dcxy', spread, near, preferred_element_type=jnp.floa...  15.6 us
    dot_general x1, matrix products, shards(): jnp.dot(x_inverse, lines_x, preferred_element_type=jnp.float32)  7.06 us
    dot_general x1, matrix products, shards(): lax.dot_general(lines_y, y_inverse, (((1,), (1,)), ((), ())), preferred_e...  6.01 us
    add x1, other arithmetic, deposit(): near_rows + jnp.where(row_iota[None, :] == base_x[:, None] + 1, got_weigh...  4.16 us

profile of v2, /device:TPU:0, one launch (start us, length us, event | category | flops | bytes accessed | tf_op | source)
XLA Modules:
  0.0 146.5 jit_solution(2484301343172998627)
XLA Ops:
  0.0 1.0 fusion.28
  1.0 0.1 fusion.36
  1.1 1.2 fusion.23
  2.3 0.7 fusion.35
  3.2 1.6 %concatenate.4 = bf16[23,2048]{1,0:T(8,128)(2,1)S(1)} concatenate(bf16[16,2048]{1,0:T(8,128)(2,1)} %param.9, bf16[4,2048]{1,0:T(4,128)(2,1)} %param.8, bf16[1,2048]{1,0:T(2,128)(2,1)S(1)} %stack.19, bf16[1,2048]{1,0:T(2,128)(2,1)S(1)} %stack.20, bf16[1,2048]{1,0:T(2,128)(2,1)S(1)} %stack.21), dimensions={0} | concatenate | bytes 188416 | tf_op jit(solution)/shard_map/concatenate | solution.py:32
  4.8 0.4 broadcast_select_fusion
  5.2 1.3 fusion.26
  6.4 0.5 broadcast.260
  6.9 0.8 reduce.2
  7.7 0.2 copy.51
  7.9 0.3 reshape.415
  8.2 21.8 %all_to_all.24 = bf16[128,2,460]{2,1,0:T(2,128)(2,1)S(1)} all-to-all(bf16[128,2,460]{2,1,0:T(2,128)(2,1)S(1)} %reshape.415), channel_id=1, replica_groups=mesh['lon'=8,'lat'=16] {'lon','lat'}, dimensions={0} | all-to-all | bytes 471040 | tf_op jit(solution)/shard_map/all_to_all | solution.py:40
  30.0 0.4 reshape.416
  30.4 0.7 copy.22
  31.2 0.1 copy.23
  31.3 0.1 add.82
  31.4 0.1 copy.24
  31.5 0.1 broadcast_in_dim.105
  31.6 0.1 copy.27
  31.8 0.1 broadcast_in_dim.112
  31.9 0.1 copy.26
  32.0 0.1 broadcast_in_dim.110
  32.1 0.1 copy.25
  32.2 0.1 broadcast_in_dim.108
  32.4 0.1 copy.28
  32.4 0.1 reshape.410
  32.6 0.3 copy.29
  32.8 0.7 broadcast_in_dim.115
  33.6 1.2 iota_compare_fusion.2
  34.8 4.2 %fusion.13 = (bf16[5120,1,288]{0,2,1:T(8,128)(2,1)S(1)}, bf16[5120,1,288]{0,2,1:T(8,128)(2,1)}) fusion(s32[5120]{0:T(1024)S(1)} %broadcast_add_fusion, s32[5120]{0:T(1024)S(1)} %add.82, bf16[5120]{0:T(1024)(128)(2,1)S(1)} %broadcast_in_dim.108, bf16[5120]{0:T(1024)(128)(2,1)S(1)} %broadcast_in_dim.105, bf16[5120]{0:T(1024)(128)(2,1)S(1)} %broadcast_in_dim.112, ...), kind=kLoop, calls=%fused_computation.18 | loop fusion | flops 20643840 | bytes 5980160 | tf_op jit(solution)/shard_map/add | solution.py:58
  38.9 15.6 %fusion.17 = f32[2,16,288,128]{3,2,1,0:T(8,128)} fusion(pred[128,5120]{1,0:T(8,128)(4,1)} %iota_compare_fusion.2, bf16[16,5120]{1,0:T(8,128)(2,1)S(1)} %broadcast_in_dim.115, bf16[5120,1,288]{0,2,1:T(8,128)(2,1)} %get-tuple-element.11, bf16[5120,1,288]{0,2,1:T(8,128)(2,1)S(1)} %get-tuple-element.10), kind=kOutput, calls=%fused_computation.26 | convolution fusion | flops 12101877760 | bytes 11436032 | tf_op jit(solution)/shard_map/cyo,odx->dcxy/dot_general | solution.py:68
  54.5 2.0 %slice_bitcast_fusion = f32[16,288,127]{2,1,0:T(8,128)S(1)} fusion(f32[2,16,288,128]{3,2,1,0:T(8,128)} %fusion.17), kind=kLoop, calls=%fused_computation.22 | loop fusion | bytes 4681728 | tf_op jit(solution)/shard_map/squeeze | solution.py:69
  56.5 1.1 copy-done
  57.6 0.7 fusion.16
  58.2 1.0 copy.50
  59.2 0.8 reshape.402
  60.0 19.8 %all_to_all.25 = bf16[8,288,256]{2,1,0:T(8,128)(2,1)S(1)} all-to-all(bf16[8,288,256]{2,1,0:T(8,128)(2,1)S(1)} %reshape.402), channel_id=1, replica_groups=mesh['lon'=8,'lat'=16] {'lon'}, dimensions={0} | all-to-all | bytes 2359296 | tf_op jit(solution)/shard_map/all_to_all | solution.py:90
  79.8 7.1 %fusion.12 = bf16[2304,256]{0,1:T(8,128)(2,1)S(1)} fusion(bf16[2304,256]{1,0:T(8,128)(2,1)S(1)} %bitcast.76, bf16[2304,2304]{1,0:T(8,128)(2,1)} %param.10), kind=kOutput, calls=%fused_computation.17 | convolution fusion | flops 2718498816 | bytes 12976128 | tf_op jit(solution)/shard_map/dot_general | solution.py:91
  86.9 0.6 copy.31
  87.5 0.1 copy.32
  87.6 0.7 copy.33
  88.3 28.7 %all_to_all.26 = bf16[128,18,256]{2,1,0:T(8,128)(2,1)S(1)} all-to-all(bf16[128,18,256]{2,1,0:T(8,128)(2,1)S(1)} %copy.33), channel_id=1, replica_groups=mesh['lon'=8,'lat'=16] {'lon','lat'}, dimensions={0} | all-to-all | bytes 2359296 | tf_op jit(solution)/shard_map/all_to_all | solution.py:95
  117.0 0.6 reshape.414
  117.6 0.2 copy.35
  117.8 6.0 %fusion.20 = bf16[36,16,8,128]{3,2,1,0:T(8,128)(2,1)S(1)} fusion(bf16[2048,2048]{1,0:T(8,128)(2,1)} %param.11, bf16[36,8,16,128]{3,2,1,0:T(8,128)(2,1)S(1)} %bitcast.77), kind=kOutput, calls=%fused_computation.27 | convolution fusion | flops 2416508928 | bytes 10747904 | tf_op jit(solution)/shard_map/dot_general | solution.py:98
  123.8 0.2 copy.49
  124.0 21.0 %all_to_all.27 = bf16[288,16,128]{2,0,1:T(8,128)(2,1)S(1)} all-to-all(bf16[288,16,128]{2,0,1:T(8,128)(2,1)S(1)} %bitcast.72), channel_id=1, replica_groups=mesh['lon'=8,'lat'=16] {'lat'}, dimensions={1} | all-to-all | bytes 2359296 | tf_op jit(solution)/shard_map/all_to_all | solution.py:102
  145.0 1.5 %copy.37 = bf16[288,16,128]{2,1,0:T(8,128)(2,1)} copy(bf16[288,16,128]{2,0,1:T(8,128)(2,1)S(1)} %all_to_all.27) | data formatting | bytes 2359296 | tf_op jit(solution)/shard_map/all_to_all | solution.py:102
  (12 shorter events, 0.1 us)
Async XLA Ops:
  0.0 5.1 %copy-start.1 = (s32[2048]{0:T(1024)S(1)}, s32[2048]{0:T(1024)}, u32[]{:S(2)}) copy-start(s32[2048]{0:T(1024)} %param.6) | copy-start | bytes 24580
  54.5 3.0 %copy-start = (f32[2,16,288,128]{3,2,1,0:T(8,128)S(1)}, f32[2,16,288,128]{3,2,1,0:T(8,128)}, u32[]{:S(2)}) copy-start(f32[2,16,288,128]{3,2,1,0:T(8,128)} %fusion.17) | copy-start | bytes 14155780

commit v3 on v1

--- a/solution.py
+++ b/solution.py
@@ -86,10 +86,13 @@
     increment = deposit(got, channels, tile_rows, tile_cols)
     pair = channels // lon_count
     lanes = pair * tile_cols
-    by_pair = increment.reshape(lon_count, pair, tile_rows, tile_cols).transpose(0, 2, 1, 3)
-    by_pair = by_pair.reshape(lon_count, tile_rows, lanes)
-    lines_x = lax.all_to_all(by_pair, "lon", 0, 0, tiled=True).reshape(line_x, lanes)
-    solved_x = jnp.dot(x_inverse, lines_x, preferred_element_type=jnp.float32).astype(jnp.bfloat16)
+    lines_x = lax.all_to_all(increment, "lon", 0, 0, tiled=True)
+    lines_x = lines_x.reshape(lon_count, pair, tile_rows, tile_cols)
+    x_blocks = x_inverse.reshape(line_x, lon_count, tile_rows)
+    solved_x = lax.dot_general(
+        x_blocks, lines_x, (((1, 2), (0, 2)), ((), ())), preferred_element_type=jnp.float32
+    )
+    solved_x = solved_x.astype(jnp.bfloat16).reshape(line_x, lanes)
     stride = tile_rows // lat_count
     by_row = solved_x.reshape(lon_count, stride, lat_count, lanes).transpose(0, 2, 1, 3)
     by_row = by_row.reshape(devices, stride, lanes)

time: 139 us -> 141 us (1.014)
  blocking collectives: 91.3 us -> 71.3 us
  local copies, waits for them, and re-layouts: 11.7 us -> 25.9 us
  starting transfers between devices: 0 us -> 3.79 us
  waiting for transfers between devices: 0 us -> 2.59 us
    all_to_all x1 -> x0, blocking collectives: 19.8 us -> none  [shards(): lax.all_to_all(by_pair, 'lon', 0, 0, tiled=True).reshape(line_x, lanes)]
    unnamed x5 -> x6, local copies, waits for them, and re-layouts: 0.82 us -> 15.3 us
    all_to_all x0 -> x1, starting transfers between devices: none -> 3.79 us  [shards(): lines_x = lax.all_to_all(increment, 'lon', 0, 0, tiled=True)]
    all_to_all x0 -> x1, waiting for transfers between devices: none -> 2.59 us  [shards(): lines_x = lax.all_to_all(increment, 'lon', 0, 0, tiled=True)]
    reshape x2 -> x0, local copies, waits for them, and re-layouts: 1.77 us -> none  [the longest x1 0.98 us: shards(): increment.reshape(lon_count, pair, tile_rows, tile_cols)]
  transfers between devices with their start and end apart: 0 -> 1, of which waited for: 0 -> 1; matrix products, arithmetic and copies ran while one was open for 0% -> 10% of each run, Pallas kernels for 0% -> 0%
where the time goes in v3:
time: 141 us; the launch traced here: 140 us
  blocking collectives  71.3 us (51%)
  matrix products  32.5 us (23%)
  local copies, waits for them, and re-layouts  25.9 us (18%)
  starting transfers between devices  3.79 us (3%)
  other arithmetic  3.65 us (3%)
  waiting for transfers between devices  2.59 us (2%)
    all_to_all x1, blocking collectives, shards(): got = lax.all_to_all(by_row, ('lon', 'lat'), 0, 0, tiled=True)  28.5 us
    all_to_all x1, blocking collectives, route_obs(): got = lax.all_to_all(send, ('lon', 'lat'), 0, 0, tiled=True)  21.8 us
    all_to_all x1, blocking collectives, shards(): tiles = lax.all_to_all(solved_y, 'lat', 1, 1, tiled=True)  21 us
    dot_general x2, matrix products, deposit(): jnp.einsum('cyo,ox->cxy', spread, near_rows, preferred_element_type=jnp.f...  16.9 us
    unnamed x6, local copies, waits for them, and re-layouts  15.3 us
    dot_general x1, matrix products, shards(): lax.dot_general(x_blocks, lines_x, (((1, 2), (0, 2)), ((), ())), preferre...  6.96 us
    dot_general x1, matrix products, shards(): lax.dot_general(lines_y, y_inverse, (((1,), (1,)), ((), ())), preferred_e...  6.07 us
    all_to_all x1, starting transfers between devices, shards(): lines_x = lax.all_to_all(increment, 'lon', 0, 0, tiled=True)  3.79 us
  transfers between devices with their start and end apart: 1, of which 1 were waited for; matrix products, arithmetic and copies ran while one was open for 10% of the time, Pallas kernels for 0%

profile of v3, /device:TPU:0, one launch (start us, length us, event | category | flops | bytes accessed | tf_op | source)
XLA Modules:
  0.0 140.0 jit_solution(10999101989616194854)
XLA Ops:
  0.0 1.0 fusion.51
  1.0 0.1 fusion.59
  1.1 1.2 fusion.46
  2.3 0.7 fusion.58
  3.2 1.6 %concatenate.4 = bf16[23,2048]{1,0:T(8,128)(2,1)S(1)} concatenate(bf16[16,2048]{1,0:T(8,128)(2,1)} %param.9, bf16[4,2048]{1,0:T(4,128)(2,1)} %param.8, bf16[1,2048]{1,0:T(2,128)(2,1)S(1)} %stack.14, bf16[1,2048]{1,0:T(2,128)(2,1)S(1)} %stack.15, bf16[1,2048]{1,0:T(2,128)(2,1)S(1)} %stack.16), dimensions={0} | concatenate | bytes 188416 | tf_op jit(solution)/shard_map/concatenate | solution.py:32
  4.8 0.4 broadcast_select_fusion
  5.1 0.0 copy-done
  5.2 1.3 fusion.49
  6.4 0.5 broadcast.125
  6.9 0.8 reduce.2
  7.7 0.2 copy.52
  7.9 0.3 reshape.211
  8.2 21.8 %all_to_all.24 = bf16[128,2,460]{2,1,0:T(2,128)(2,1)S(1)} all-to-all(bf16[128,2,460]{2,1,0:T(2,128)(2,1)S(1)} %reshape.211), channel_id=1, replica_groups=mesh['lon'=8,'lat'=16] {'lon','lat'}, dimensions={0} | all-to-all | bytes 471040 | tf_op jit(solution)/shard_map/all_to_all | solution.py:40
  30.0 0.4 reshape.212
  30.4 0.7 copy.25
  31.2 0.1 copy.29
  31.3 0.1 reshape.204
  31.4 0.3 iota_compare_fusion.3
  31.7 0.1 copy.26
  31.8 0.1 add.75
  32.0 0.1 copy.27
  32.1 0.1 broadcast_in_dim.117
  32.2 0.1 copy.31
  32.3 0.1 broadcast_in_dim.126
  32.4 0.1 copy.28
  32.6 0.1 broadcast_in_dim.120
  32.7 0.1 copy.32
  32.8 0.1 broadcast_in_dim.128
  32.9 0.3 copy.30
  33.2 0.7 broadcast_in_dim.123
  33.9 0.3 iota_compare_fusion.2
  34.3 7.9 %fusion = f32[288,16,128]{2,0,1:T(8,128)} fusion(pred[128,5120]{1,0:T(8,128)(4,1)S(1)} %iota_compare_fusion.2, bf16[16,5120]{1,0:T(8,128)(2,1)S(1)} %broadcast_in_dim.123, s32[5120]{0:T(1024)S(1)} %broadcast_add_fusion.1, s32[5120]{0:T(1024)S(1)} %add.75, bf16[5120]{0:T(1024)(128)(2,1)S(1)} %broadcast_in_dim.128, bf16[5120]{0:T(1024)(128)(2,1)S(1)} %broadcast_in_dim.126), kind=kOutput, calls=%fused_computation | convolution fusion | flops 6062080000 | bytes 3239936 | tf_op jit(solution)/shard_map/cyo,ox->cxy/dot_general | solution.py:68
  42.2 8.9 %fusion.38 = bf16[16,288,128]{2,1,0:T(8,128)(2,1)} fusion(f32[288,16,128]{2,0,1:T(8,128)} %fusion, pred[128,5120]{1,0:T(8,128)(4,1)S(1)} %iota_compare_fusion.3, bf16[16,5120]{1,0:T(8,128)(2,1)S(1)} %broadcast_in_dim.123, s32[5120]{0:T(1024)S(1)} %broadcast_add_fusion.1, s32[5120]{0:T(1024)S(1)} %add.75, bf16[5120]{0:T(1024)(128)(2,1)S(1)} %broadcast_in_dim.120, ...), kind=kOutput, calls=%fused_computation.38 | convolution fusion | flops 6063259648 | bytes 4419584 | tf_op jit(solution)/shard_map/cyo,ox->cxy/dot_general | solution.py:68
  51.2 3.8 %all-to-all-start.1 = ((bf16[16,288,128]{2,1,0:T(8,128)(2,1)}), bf16[16,288,128]{2,1,0:T(8,128)(2,1)S(1)}, u32[]{:S(2)}, u32[]{:S(2)}) async-start(bf16[16,288,128]{2,1,0:T(8,128)(2,1)} %fusion.38), calls=%async_computation.1 | async-start | bytes 2359296 | tf_op jit(solution)/shard_map/all_to_all | solution.py:89
  55.0 14.5 %copy.33 = bf16[2304,2304]{0,1:T(8,128)(2,1)} copy(bf16[2304,2304]{1,0:T(8,128)(2,1)} %param.10) | data formatting | bytes 21233664 | tf_op args[4]
  69.4 2.6 %all-to-all-done.1 = bf16[16,288,128]{2,1,0:T(8,128)(2,1)S(1)} async-done(((bf16[16,288,128]{2,1,0:T(8,128)(2,1)}), bf16[16,288,128]{2,1,0:T(8,128)(2,1)S(1)}, u32[]{:S(2)}, u32[]{:S(2)}) %all-to-all-start.1) | async-done | bytes 1179680 | tf_op jit(solution)/shard_map/all_to_all | solution.py:89
  72.0 7.0 %fusion.15 = bf16[2304,2,128]{0,2,1:T(8,128)(2,1)S(1)} fusion(bf16[8,2,288,128]{3,2,1,0:T(8,128)(2,1)S(1)} %bitcast.70, bf16[2304,8,288,1]{0,2,3,1:T(8,128)(2,1)} %bitcast.65), kind=kOutput, calls=%fused_computation.19 | convolution fusion | flops 2718498816 | bytes 12976128 | tf_op jit(solution)/shard_map/dot_general | solution.py:92
  79.0 1.4 %copy.34 = bf16[2304,2,128]{2,1,0:T(2,128)(2,1)S(1)} copy(bf16[2304,2,128]{0,2,1:T(8,128)(2,1)S(1)} %fusion.15) | data formatting | bytes 2359296 | tf_op jit(solution)/shard_map/convert_element_type | solution.py:95
  80.4 0.8 reshape_reshape.3
  81.2 0.1 copy.35
  81.3 0.7 copy.36
  82.0 28.5 %all_to_all.25 = bf16[128,18,256]{2,1,0:T(8,128)(2,1)S(1)} all-to-all(bf16[128,18,256]{2,1,0:T(8,128)(2,1)S(1)} %copy.36), channel_id=1, replica_groups=mesh['lon'=8,'lat'=16] {'lon','lat'}, dimensions={0} | all-to-all | bytes 2359296 | tf_op jit(solution)/shard_map/all_to_all | solution.py:99
  110.5 0.6 reshape.210
  111.1 0.2 copy.38
  111.3 6.1 %fusion.43 = bf16[36,16,8,128]{3,2,1,0:T(8,128)(2,1)S(1)} fusion(bf16[2048,2048]{1,0:T(8,128)(2,1)} %param.11, bf16[36,8,16,128]{3,2,1,0:T(8,128)(2,1)S(1)} %bitcast.71), kind=kOutput, calls=%fused_computation.39 | convolution fusion | flops 2416508928 | bytes 10747904 | tf_op jit(solution)/shard_map/dot_general | solution.py:102
  117.3 0.2 copy.51
  117.6 21.0 %all_to_all.26 = bf16[288,16,128]{2,0,1:T(8,128)(2,1)S(1)} all-to-all(bf16[288,16,128]{2,0,1:T(8,128)(2,1)S(1)} %bitcast.67), channel_id=1, replica_groups=mesh['lon'=8,'lat'=16] {'lat'}, dimensions={1} | all-to-all | bytes 2359296 | tf_op jit(solution)/shard_map/all_to_all | solution.py:106
  138.6 1.5 %copy.40 = bf16[288,16,128]{2,1,0:T(8,128)(2,1)} copy(bf16[288,16,128]{2,0,1:T(8,128)(2,1)S(1)} %all_to_all.26) | data formatting | bytes 2359296 | tf_op jit(solution)/shard_map/all_to_all | solution.py:106
  (11 shorter events, 0.1 us)
Async XLA Ops:
  0.0 5.1 %copy-start = (s32[2048]{0:T(1024)S(1)}, s32[2048]{0:T(1024)}, u32[]{:S(2)}) copy-start(s32[2048]{0:T(1024)} %param.6) | copy-start | bytes 24580
  51.2 20.8 %all-to-all-start.1 = ((bf16[16,288,128]{2,1,0:T(8,128)(2,1)}), bf16[16,288,128]{2,1,0:T(8,128)(2,1)S(1)}, u32[]{:S(2)}, u32[]{:S(2)}) async-start(bf16[16,288,128]{2,1,0:T(8,128)(2,1)} %fusion.38), calls=%async_computation.1 | async-start | bytes 2359296 | tf_op jit(solution)/shard_map/all_to_all | solution.py:89

commit v4 on v2

--- a/solution.py
+++ b/solution.py
@@ -2,6 +2,8 @@
 import jax.numpy as jnp
 from jax import lax
 from jax.sharding import PartitionSpec as P
+from jax.experimental import pallas as pl
+from jax.experimental.pallas import tpu as pltpu
 
 
 def tile_ranks(owner_tile, groups):
@@ -42,32 +44,72 @@
     return got
 
 
+def deposit_kernel(vals_ref, by_ref, bx_ref, w_ref, out_ref, acc_ref, spread_ref):
+    step = pl.program_id(0)
+    chunk, channels = vals_ref.shape
+    tile_rows = out_ref.shape[0]
+    tile_cols = out_ref.shape[1] // channels
+
+    @pl.when(step == 0)
+    def _():
+        acc_ref[...] = jnp.zeros_like(acc_ref)
+
+    zero = jnp.zeros((), jnp.bfloat16)
+    lane_y = lax.broadcasted_iota(jnp.int32, (chunk, tile_cols), 1)
+    hit_y = lane_y == by_ref[...]
+    for c in range(channels):
+        spread_ref[:, c * tile_cols : (c + 1) * tile_cols] = jnp.where(
+            hit_y, vals_ref[:, c : c + 1], zero
+        )
+    row_x = lax.broadcasted_iota(jnp.int32, (tile_rows, chunk), 0)
+    base_x = bx_ref[...]
+    at_x = row_x == base_x
+    next_x = row_x == base_x + 1
+    for offset_y in range(2):
+        near = jnp.where(at_x, w_ref[2 * offset_y : 2 * offset_y + 1, :], zero) + jnp.where(
+            next_x, w_ref[2 * offset_y + 1 : 2 * offset_y + 2, :], zero
+        )
+        acc_ref[offset_y] += jnp.dot(near, spread_ref[...], preferred_element_type=jnp.float32)
+
+    @pl.when(step == pl.num_programs(0) - 1)
+    def _():
+        later = pltpu.roll(acc_ref[1], 1, 1)
+        lane = lax.broadcasted_iota(jnp.int32, later.shape, 1)
+        later = jnp.where(lane % tile_cols == 0, 0.0, later)
+        out_ref[...] = (acc_ref[0] + later).astype(out_ref.dtype)
+
+
 def deposit(got, channels, tile_rows, tile_cols):
-    values = got[:channels]
-    got_weights = got[channels : channels + 4]
-    base_y = got[channels + 4].astype(jnp.int32)
-    base_x = got[channels + 5].astype(jnp.int32) + 128 * got[channels + 6].astype(jnp.int32)
-    row_iota = jnp.arange(tile_rows, dtype=jnp.int32)
-    col_iota = jnp.arange(tile_cols, dtype=jnp.int32)
-    zero_value = jnp.zeros((), jnp.bfloat16)
-    near = []
-    for offset_y in range(2):
-        near_rows = jnp.where(
-            row_iota[None, :] == base_x[:, None], got_weights[2 * offset_y][:, None], zero_value
-        )
-        near_rows = near_rows + jnp.where(
-            row_iota[None, :] == base_x[:, None] + 1,
-            got_weights[2 * offset_y + 1][:, None],
-            zero_value,
-        )
-        near.append(near_rows)
-    near = jnp.stack(near, 1)
-    spread = jnp.where(
-        col_iota[None, :, None] == base_y[None, None, :], values[:, None, :], zero_value
-    )
-    both = jnp.einsum("cyo,odx->dcxy", spread, near, preferred_element_type=jnp.float32)
-    shifted = jnp.pad(both[1, :, :, :-1], ((0, 0), (0, 0), (1, 0)))
-    return (both[0] + shifted).astype(jnp.bfloat16)
+    obs = got.shape[1]
+    chunk = 512
+    vals_col = got[:channels].T
+    by_col = got[channels + 4].astype(jnp.int32)[:, None]
+    bx_row = (got[channels + 5].astype(jnp.int32) + 128 * got[channels + 6].astype(jnp.int32))[None, :]
+    w_row = got[channels : channels + 4]
+    lanes = channels * tile_cols
+    return pl.pallas_call(
+        deposit_kernel,
+        out_shape=jax.ShapeDtypeStruct((tile_rows, lanes), jnp.bfloat16),
+        grid=(obs // chunk,),
+        in_specs=[
+            pl.BlockSpec((chunk, channels), lambda k: (k, 0)),
+            pl.BlockSpec((chunk, 1), lambda k: (k, 0)),
+            pl.BlockSpec((1, chunk), lambda k: (0, k)),
+            pl.BlockSpec((4, chunk), lambda k: (0, k)),
+        ],
+        out_specs=pl.BlockSpec((tile_rows, lanes), lambda k: (0, 0)),
+        scratch_shapes=[
+            pltpu.VMEM((2, tile_rows, lanes), jnp.float32),
+            pltpu.VMEM((chunk, lanes), jnp.bfloat16),
+        ],
+        compiler_params=pltpu.CompilerParams(
+            dimension_semantics=("arbitrary",), vmem_limit_bytes=48 * 1024 * 1024
+        ),
+        cost_estimate=pl.CostEstimate(
+            flops=4 * tile_rows * lanes * obs, bytes_accessed=obs * 48 + tile_rows * lanes * 2,
+            transcendentals=0,
+        ),
+    )(vals_col, by_col, bx_row, w_row)
 
 
 def shards(owner_tile, corner_cell, weights, innovations, x_inverse, y_inverse):
@@ -85,8 +127,7 @@
     increment = deposit(got, channels, tile_rows, tile_cols)
     pair = channels // lon_count
     lanes = pair * tile_cols
-    by_pair = increment.reshape(lon_count, pair, tile_rows, tile_cols).transpose(0, 2, 1, 3)
-    by_pair = by_pair.reshape(lon_count, tile_rows, lanes)
+    by_pair = increment.reshape(tile_rows, lon_count, lanes).transpose(1, 0, 2)
     lines_x = lax.all_to_all(by_pair, "lon", 0, 0, tiled=True).reshape(line_x, lanes)
     solved_x = jnp.dot(x_inverse, lines_x, preferred_element_type=jnp.float32).astype(jnp.bfloat16)
     stride = tile_rows // lat_count

time: 147 us -> 151 us (1.027)
  Pallas kernels: 0 us -> 30 us
  matrix products: 31.2 us -> 15.7 us
  other arithmetic: 8.97 us -> 2.21 us
  local copies, waits for them, and re-layouts: 14.7 us -> 10.7 us
    pallas_call x0 -> x1, Pallas kernels: none -> 30 us  [deposit(): pl.pallas_call(deposit_kernel, out_shape=jax.ShapeDtypeStruct((tile_rows,...]
    dot_general x1 -> x0, matrix products: 15.6 us -> none  [deposit(): jnp.einsum('cyo,odx->dcxy', spread, near, preferred_element_type=jnp.floa...]
    add x2 -> x0, other arithmetic: 4.17 us -> none  [the longest x1 4.16 us: deposit(): near_rows + jnp.where(row_iota[None, :] == base_x[:, None] + 1, got_weigh...]
    squeeze x1 -> x0, local copies, waits for them, and re-layouts: 1.98 us -> none  [deposit(): shifted = jnp.pad(both[1, :, :, :-1], ((0, 0), (0, 0), (1, 0)))]
    reshape x2 -> x1, local copies, waits for them, and re-layouts: 1.77 us -> 0.08 us  [shards(): by_pair = increment.reshape(tile_rows, lon_count, lanes).transpose(1, 0, 2)]
    concatenate x1, local copies, waits for them, and re-layouts: 1.61 us -> 0.06 us  [route_obs(): stacked = jnp.concatenate([innovations, weights, digits], 0)]
where the time goes in v4:
time: 151 us; the launch traced here: 150 us
  blocking collectives  91.3 us (60%)
  Pallas kernels  30 us (20%)
  matrix products  15.7 us (10%)
  local copies, waits for them, and re-layouts  10.7 us (7%)
  other arithmetic  2.21 us (1%)
    pallas_call x1, Pallas kernels, deposit(): pl.pallas_call(deposit_kernel, out_shape=jax.ShapeDtypeStruct((tile_rows,...  30 us
    all_to_all x1, blocking collectives, shards(): got = lax.all_to_all(by_row, ('lon', 'lat'), 0, 0, tiled=True)  28.7 us
    all_to_all x1, blocking collectives, route_obs(): got = lax.all_to_all(send, ('lon', 'lat'), 0, 0, tiled=True)  21.8 us
    all_to_all x1, blocking collectives, shards(): tiles = lax.all_to_all(solved_y, 'lat', 1, 1, tiled=True)  21 us
    all_to_all x1, blocking collectives, shards(): lax.all_to_all(by_pair, 'lon', 0, 0, tiled=True).reshape(line_x, lanes)  19.8 us
    dot_general x1, matrix products, shards(): jnp.dot(x_inverse, lines_x, preferred_element_type=jnp.float32)  7.06 us
    dot_general x1, matrix products, shards(): lax.dot_general(lines_y, y_inverse, (((1,), (1,)), ((), ())), preferred_e...  6.02 us

profile of v4, /device:TPU:0, one launch (start us, length us, event | category | flops | bytes accessed | tf_op | source)
XLA Modules:
  0.0 150.1 jit_solution(249485243932849468)
XLA Ops:
  0.0 0.0 copy-start.4
  0.0 0.0 copy-start.1
  0.0 0.0 copy-start.3
  0.0 1.0 fusion.9
  1.0 0.1 fusion.17
  1.1 1.2 fusion.4
  2.3 0.0 copy-done.4
  2.4 0.0 copy-done.1
  2.5 0.0 copy-done.3
  2.5 0.1 concatenate.4
  2.5 0.0 copy-start.2
  2.5 0.4 broadcast_select_fusion
  2.9 0.3 copy-done.2
  3.2 1.3 fusion.7
  4.5 0.5 broadcast.77
  5.0 0.8 reduce.2
  5.8 0.2 copy.55
  6.0 0.3 reshape.157
  6.2 21.8 %all_to_all.24 = bf16[128,2,460]{2,1,0:T(2,128)(2,1)S(1)} all-to-all(bf16[128,2,460]{2,1,0:T(2,128)(2,1)S(1)} %reshape.157), channel_id=1, replica_groups=mesh['lon'=8,'lat'=16] {'lon','lat'}, dimensions={0} | all-to-all | bytes 471040 | tf_op jit(solution)/shard_map/all_to_all | solution.py:42
  28.1 0.4 reshape.158
  28.5 0.7 copy.28
  29.3 0.1 copy.30
  29.4 0.1 copy.31
  29.5 0.1 add.48.bx_ref
  29.6 0.1 copy.32
  29.7 0.2 slice.30.w_ref
  29.9 1.7 %copy.29 = bf16[16,128,40]{0,2,1:T(8,128)(2,1)} copy(bf16[16,128,40]{1,2,0:T(8,128)(2,1)S(1)} %slice.31) | data formatting | bytes 327680 | tf_op jit(solution)/shard_map/slice | solution.py:85
  31.6 0.7 reshape.155.by_ref
  32.3 0.0 copy-start
  32.4 1.3 copy-done
  33.7 30.0 %shard_map.64 = bf16[288,2048]{1,0:T(8,128)(2,1)S(1)} custom-call(bf16[5120,16]{1,0:T(8,128)(2,1)S(1)} %bitcast.53, s32[5120,1]{1,0:T(8,128)S(1)} %reshape.155.by_ref, s32[1,5120]{1,0:T(1,128)S(1)} %add.48.bx_ref, bf16[4,5120]{1,0:T(4,128)(2,1)S(1)} %slice.30.w_ref), custom_call_target="tpu_custom_call" | custom-call | flops 12079595520 | bytes 1425408 | tf_op jit(solution)/shard_map/pallas_call | solution.py:90
  63.6 0.1 copy.54
  63.7 19.8 %all_to_all.25 = bf16[8,288,256]{2,1,0:T(8,128)(2,1)S(1)} all-to-all(bf16[8,288,256]{2,1,0:T(8,128)(2,1)S(1)} %bitcast.56), channel_id=1, replica_groups=mesh['lon'=8,'lat'=16] {'lon'}, dimensions={0} | all-to-all | bytes 2359296 | tf_op jit(solution)/shard_map/all_to_all | solution.py:131
  83.5 7.1 %fusion = bf16[2304,256]{0,1:T(8,128)(2,1)S(1)} fusion(bf16[2304,256]{1,0:T(8,128)(2,1)S(1)} %bitcast.61, bf16[2304,2304]{1,0:T(8,128)(2,1)} %param.10), kind=kOutput, calls=%fused_computation.2 | convolution fusion | flops 2718498816 | bytes 12976128 | tf_op jit(solution)/shard_map/dot_general | solution.py:132
  90.6 0.6 copy.35
  91.2 0.1 copy.36
  91.3 0.7 copy.37
  92.0 28.7 %all_to_all.26 = bf16[128,18,256]{2,1,0:T(8,128)(2,1)S(1)} all-to-all(bf16[128,18,256]{2,1,0:T(8,128)(2,1)S(1)} %copy.37), channel_id=1, replica_groups=mesh['lon'=8,'lat'=16] {'lon','lat'}, dimensions={0} | all-to-all | bytes 2359296 | tf_op jit(solution)/shard_map/all_to_all | solution.py:136
  120.7 0.6 reshape.156
  121.3 0.2 copy.39
  121.4 6.0 %fusion.1 = bf16[36,16,8,128]{3,2,1,0:T(8,128)(2,1)S(1)} fusion(bf16[2048,2048]{1,0:T(8,128)(2,1)} %param.11, bf16[36,8,16,128]{3,2,1,0:T(8,128)(2,1)S(1)} %bitcast.62), kind=kOutput, calls=%fused_computation.4 | convolution fusion | flops 2416508928 | bytes 10747904 | tf_op jit(solution)/shard_map/dot_general | solution.py:139
  127.5 0.2 copy.53
  127.7 21.0 %all_to_all.27 = bf16[288,16,128]{2,0,1:T(8,128)(2,1)S(1)} all-to-all(bf16[288,16,128]{2,0,1:T(8,128)(2,1)S(1)} %bitcast.58), channel_id=1, replica_groups=mesh['lon'=8,'lat'=16] {'lat'}, dimensions={1} | all-to-all | bytes 2359296 | tf_op jit(solution)/shard_map/all_to_all | solution.py:143
  148.7 1.5 copy.41
  (10 shorter events, 0.1 us)
Async XLA Ops:
  0.0 2.3 %copy-start.4 = (s32[2048]{0:T(1024)S(1)}, s32[2048]{0:T(1024)}, u32[]{:S(2)}) copy-start(s32[2048]{0:T(1024)} %param.7) | copy-start | bytes 24580
  0.0 2.4 %copy-start.1 = (bf16[16,2048]{1,0:T(8,128)(2,1)S(1)}, bf16[16,2048]{1,0:T(8,128)(2,1)}, u32[]{:S(2)}) copy-start(bf16[16,2048]{1,0:T(8,128)(2,1)} %param.9) | copy-start | bytes 196612
  0.0 2.4 %copy-start.3 = (bf16[4,2048]{1,0:T(4,128)(2,1)S(1)}, bf16[4,2048]{1,0:T(4,128)(2,1)}, u32[]{:S(2)}) copy-start(bf16[4,2048]{1,0:T(4,128)(2,1)} %param.8) | copy-start | bytes 49156
  2.5 0.7 copy-start.2
  32.3 1.3 copy-start

commit v5 on v4

--- a/solution.py
+++ b/solution.py
@@ -81,7 +81,7 @@
 
 def deposit(got, channels, tile_rows, tile_cols):
     obs = got.shape[1]
-    chunk = 512
+    chunk = 2560
     vals_col = got[:channels].T
     by_col = got[channels + 4].astype(jnp.int32)[:, None]
     bx_row = (got[channels + 5].astype(jnp.int32) + 128 * got[channels + 6].astype(jnp.int32))[None, :]

time: 151 us -> 146 us (0.967)
  Pallas kernels: 30 us -> 25.8 us
    pallas_call x1, Pallas kernels: 30 us -> 25.8 us  [deposit(): pl.pallas_call(deposit_kernel, out_shape=jax.ShapeDtypeStruct((tile_rows,...]
where the time goes in v5:
time: 146 us
  blocking collectives  91.3 us (63%)
  Pallas kernels  25.8 us (18%)
  matrix products  15.7 us (11%)
  local copies, waits for them, and re-layouts  10.7 us (7%)
  other arithmetic  2.21 us (2%)
    all_to_all x1, blocking collectives, shards(): got = lax.all_to_all(by_row, ('lon', 'lat'), 0, 0, tiled=True)  28.7 us
    pallas_call x1, Pallas kernels, deposit(): pl.pallas_call(deposit_kernel, out_shape=jax.ShapeDtypeStruct((tile_rows,...  25.8 us
    all_to_all x1, blocking collectives, route_obs(): got = lax.all_to_all(send, ('lon', 'lat'), 0, 0, tiled=True)  21.8 us
    all_to_all x1, blocking collectives, shards(): tiles = lax.all_to_all(solved_y, 'lat', 1, 1, tiled=True)  21 us
    all_to_all x1, blocking collectives, shards(): lax.all_to_all(by_pair, 'lon', 0, 0, tiled=True).reshape(line_x, lanes)  19.8 us
    dot_general x1, matrix products, shards(): jnp.dot(x_inverse, lines_x, preferred_element_type=jnp.float32)  7.06 us
    dot_general x1, matrix products, shards(): lax.dot_general(lines_y, y_inverse, (((1,), (1,)), ((), ())), preferred_e...  6.02 us

profile of v5, /device:TPU:0, one launch (start us, length us, event | category | flops | bytes accessed | tf_op | source)
XLA Modules:
  0.0 146.0 jit_solution(12679139887162861628)
XLA Ops:
  0.0 0.0 copy-start.4
  0.0 0.0 copy-start.1
  0.0 0.0 copy-start.3
  0.0 1.0 fusion.9
  1.0 0.1 fusion.17
  1.1 1.2 fusion.4
  2.3 0.0 copy-done.4
  2.4 0.0 copy-done.1
  2.5 0.0 copy-done.3
  2.5 0.1 concatenate.4
  2.5 0.0 copy-start.2
  2.5 0.4 broadcast_select_fusion
  2.9 0.3 copy-done.2
  3.2 1.3 fusion.7
  4.5 0.5 broadcast.77
  5.0 0.8 reduce.2
  5.8 0.2 copy.55
  6.0 0.3 reshape.157
  6.2 21.8 %all_to_all.24 = bf16[128,2,460]{2,1,0:T(2,128)(2,1)S(1)} all-to-all(bf16[128,2,460]{2,1,0:T(2,128)(2,1)S(1)} %reshape.157), channel_id=1, replica_groups=mesh['lon'=8,'lat'=16] {'lon','lat'}, dimensions={0} | all-to-all | bytes 471040 | tf_op jit(solution)/shard_map/all_to_all | solution.py:42
  28.1 0.4 reshape.158
  28.5 0.7 copy.28
  29.3 0.1 copy.30
  29.4 0.1 copy.31
  29.5 0.1 add.48.bx_ref
  29.6 0.1 copy.32
  29.7 0.2 slice.30.w_ref
  29.9 1.7 %copy.29 = bf16[16,128,40]{0,2,1:T(8,128)(2,1)} copy(bf16[16,128,40]{1,2,0:T(8,128)(2,1)S(1)} %slice.31) | data formatting | bytes 327680 | tf_op jit(solution)/shard_map/slice | solution.py:85
  31.6 0.7 reshape.155.by_ref
  32.3 0.0 copy-start
  32.4 1.3 copy-done
  33.7 25.8 %shard_map.64 = bf16[288,2048]{1,0:T(8,128)(2,1)S(1)} custom-call(bf16[5120,16]{1,0:T(8,128)(2,1)S(1)} %bitcast.53, s32[5120,1]{1,0:T(8,128)S(1)} %reshape.155.by_ref, s32[1,5120]{1,0:T(1,128)S(1)} %add.48.bx_ref, bf16[4,5120]{1,0:T(4,128)(2,1)S(1)} %slice.30.w_ref), custom_call_target="tpu_custom_call" | custom-call | flops 12079595520 | bytes 1425408 | tf_op jit(solution)/shard_map/pallas_call | solution.py:90
  59.5 0.1 copy.54
  59.6 19.8 %all_to_all.25 = bf16[8,288,256]{2,1,0:T(8,128)(2,1)S(1)} all-to-all(bf16[8,288,256]{2,1,0:T(8,128)(2,1)S(1)} %bitcast.56), channel_id=1, replica_groups=mesh['lon'=8,'lat'=16] {'lon'}, dimensions={0} | all-to-all | bytes 2359296 | tf_op jit(solution)/shard_map/all_to_all | solution.py:131
  79.4 7.1 %fusion = bf16[2304,256]{0,1:T(8,128)(2,1)S(1)} fusion(bf16[2304,256]{1,0:T(8,128)(2,1)S(1)} %bitcast.61, bf16[2304,2304]{1,0:T(8,128)(2,1)} %param.10), kind=kOutput, calls=%fused_computation.2 | convolution fusion | flops 2718498816 | bytes 12976128 | tf_op jit(solution)/shard_map/dot_general | solution.py:132
  86.4 0.6 copy.35
  87.1 0.1 copy.36
  87.2 0.7 copy.37
  87.9 28.7 %all_to_all.26 = bf16[128,18,256]{2,1,0:T(8,128)(2,1)S(1)} all-to-all(bf16[128,18,256]{2,1,0:T(8,128)(2,1)S(1)} %copy.37), channel_id=1, replica_groups=mesh['lon'=8,'lat'=16] {'lon','lat'}, dimensions={0} | all-to-all | bytes 2359296 | tf_op jit(solution)/shard_map/all_to_all | solution.py:136
  116.6 0.6 reshape.156
  117.1 0.2 copy.39
  117.3 6.0 %fusion.1 = bf16[36,16,8,128]{3,2,1,0:T(8,128)(2,1)S(1)} fusion(bf16[2048,2048]{1,0:T(8,128)(2,1)} %param.11, bf16[36,8,16,128]{3,2,1,0:T(8,128)(2,1)S(1)} %bitcast.62), kind=kOutput, calls=%fused_computation.4 | convolution fusion | flops 2416508928 | bytes 10747904 | tf_op jit(solution)/shard_map/dot_general | solution.py:139
  123.3 0.2 copy.53
  123.6 21.0 %all_to_all.27 = bf16[288,16,128]{2,0,1:T(8,128)(2,1)S(1)} all-to-all(bf16[288,16,128]{2,0,1:T(8,128)(2,1)S(1)} %bitcast.58), channel_id=1, replica_groups=mesh['lon'=8,'lat'=16] {'lat'}, dimensions={1} | all-to-all | bytes 2359296 | tf_op jit(solution)/shard_map/all_to_all | solution.py:143
  144.5 1.5 %copy.41 = bf16[288,16,128]{2,1,0:T(8,128)(2,1)} copy(bf16[288,16,128]{2,0,1:T(8,128)(2,1)S(1)} %all_to_all.27) | data formatting | bytes 2359296 | tf_op jit(solution)/shard_map/all_to_all | solution.py:143
  (10 shorter events, 0.1 us)
Async XLA Ops:
  0.0 2.3 %copy-start.4 = (s32[2048]{0:T(1024)S(1)}, s32[2048]{0:T(1024)}, u32[]{:S(2)}) copy-start(s32[2048]{0:T(1024)} %param.7) | copy-start | bytes 24580
  0.0 2.4 %copy-start.1 = (bf16[16,2048]{1,0:T(8,128)(2,1)S(1)}, bf16[16,2048]{1,0:T(8,128)(2,1)}, u32[]{:S(2)}) copy-start(bf16[16,2048]{1,0:T(8,128)(2,1)} %param.9) | copy-start | bytes 196612
  0.0 2.4 %copy-start.3 = (bf16[4,2048]{1,0:T(4,128)(2,1)S(1)}, bf16[4,2048]{1,0:T(4,128)(2,1)}, u32[]{:S(2)}) copy-start(bf16[4,2048]{1,0:T(4,128)(2,1)} %param.8) | copy-start | bytes 49156
  2.5 0.7 copy-start.2
  32.3 1.3 copy-start

commit v6 on v5

--- a/solution.py
+++ b/solution.py
@@ -46,70 +46,72 @@
 
 def deposit_kernel(vals_ref, by_ref, bx_ref, w_ref, out_ref, acc_ref, spread_ref):
     step = pl.program_id(0)
-    chunk, channels = vals_ref.shape
-    tile_rows = out_ref.shape[0]
-    tile_cols = out_ref.shape[1] // channels
+    channels, chunk = vals_ref.shape
+    tile_cols = out_ref.shape[0] // channels
+    wide = out_ref.shape[1]
 
     @pl.when(step == 0)
     def _():
         acc_ref[...] = jnp.zeros_like(acc_ref)
 
     zero = jnp.zeros((), jnp.bfloat16)
-    lane_y = lax.broadcasted_iota(jnp.int32, (chunk, tile_cols), 1)
-    hit_y = lane_y == by_ref[...]
+    row_y = lax.broadcasted_iota(jnp.int32, (tile_cols, chunk), 0)
+    hit_y = row_y == by_ref[...]
     for c in range(channels):
-        spread_ref[:, c * tile_cols : (c + 1) * tile_cols] = jnp.where(
-            hit_y, vals_ref[:, c : c + 1], zero
+        spread_ref[c * tile_cols : (c + 1) * tile_cols, :] = jnp.where(
+            hit_y, vals_ref[c : c + 1, :], zero
         )
-    row_x = lax.broadcasted_iota(jnp.int32, (tile_rows, chunk), 0)
+    col_x = lax.broadcasted_iota(jnp.int32, (chunk, wide), 1)
     base_x = bx_ref[...]
-    at_x = row_x == base_x
-    next_x = row_x == base_x + 1
+    at_x = col_x == base_x
+    next_x = col_x == base_x + 1
     for offset_y in range(2):
-        near = jnp.where(at_x, w_ref[2 * offset_y : 2 * offset_y + 1, :], zero) + jnp.where(
-            next_x, w_ref[2 * offset_y + 1 : 2 * offset_y + 2, :], zero
+        near = jnp.where(at_x, w_ref[:, 2 * offset_y : 2 * offset_y + 1], zero) + jnp.where(
+            next_x, w_ref[:, 2 * offset_y + 1 : 2 * offset_y + 2], zero
         )
-        acc_ref[offset_y] += jnp.dot(near, spread_ref[...], preferred_element_type=jnp.float32)
+        acc_ref[offset_y] += jnp.dot(spread_ref[...], near, preferred_element_type=jnp.float32)
 
     @pl.when(step == pl.num_programs(0) - 1)
     def _():
-        later = pltpu.roll(acc_ref[1], 1, 1)
-        lane = lax.broadcasted_iota(jnp.int32, later.shape, 1)
-        later = jnp.where(lane % tile_cols == 0, 0.0, later)
+        later = pltpu.roll(acc_ref[1], 1, 0)
+        row = lax.broadcasted_iota(jnp.int32, later.shape, 0)
+        later = jnp.where(row % tile_cols == 0, 0.0, later)
         out_ref[...] = (acc_ref[0] + later).astype(out_ref.dtype)
 
 
 def deposit(got, channels, tile_rows, tile_cols):
     obs = got.shape[1]
-    chunk = 2560
-    vals_col = got[:channels].T
-    by_col = got[channels + 4].astype(jnp.int32)[:, None]
-    bx_row = (got[channels + 5].astype(jnp.int32) + 128 * got[channels + 6].astype(jnp.int32))[None, :]
-    w_row = got[channels : channels + 4]
+    chunk = 1280
+    wide = -(-tile_rows // 128) * 128
+    vals_row = got[:channels]
+    by_row = got[channels + 4].astype(jnp.int32)[None, :]
+    bx_col = (got[channels + 5].astype(jnp.int32) + 128 * got[channels + 6].astype(jnp.int32))[:, None]
+    w_col = got[channels : channels + 4].T
     lanes = channels * tile_cols
-    return pl.pallas_call(
+    out = pl.pallas_call(
         deposit_kernel,
-        out_shape=jax.ShapeDtypeStruct((tile_rows, lanes), jnp.bfloat16),
+        out_shape=jax.ShapeDtypeStruct((lanes, wide), jnp.bfloat16),
         grid=(obs // chunk,),
         in_specs=[
-            pl.BlockSpec((chunk, channels), lambda k: (k, 0)),
+            pl.BlockSpec((channels, chunk), lambda k: (0, k)),
+            pl.BlockSpec((1, chunk), lambda k: (0, k)),
             pl.BlockSpec((chunk, 1), lambda k: (k, 0)),
-            pl.BlockSpec((1, chunk), lambda k: (0, k)),
-            pl.BlockSpec((4, chunk), lambda k: (0, k)),
+            pl.BlockSpec((chunk, 4), lambda k: (k, 0)),
         ],
-        out_specs=pl.BlockSpec((tile_rows, lanes), lambda k: (0, 0)),
+        out_specs=pl.BlockSpec((lanes, wide), lambda k: (0, 0)),
         scratch_shapes=[
-            pltpu.VMEM((2, tile_rows, lanes), jnp.float32),
-            pltpu.VMEM((chunk, lanes), jnp.bfloat16),
+            pltpu.VMEM((2, lanes, wide), jnp.float32),
+            pltpu.VMEM((lanes, chunk), jnp.bfloat16),
         ],
         compiler_params=pltpu.CompilerParams(
             dimension_semantics=("arbitrary",), vmem_limit_bytes=48 * 1024 * 1024
         ),
         cost_estimate=pl.CostEstimate(
-            flops=4 * tile_rows * lanes * obs, bytes_accessed=obs * 48 + tile_rows * lanes * 2,
+            flops=4 * wide * lanes * obs, bytes_accessed=obs * 48 + wide * lanes * 2,
             transcendentals=0,
         ),
-    )(vals_col, by_col, bx_row, w_row)
+    )(vals_row, by_row, bx_col, w_col)
+    return out[:, :tile_rows].reshape(channels, tile_cols, tile_rows).transpose(0, 2, 1)
 
 
 def shards(owner_tile, corner_cell, weights, innovations, x_inverse, y_inverse):
@@ -127,7 +129,8 @@
     increment = deposit(got, channels, tile_rows, tile_cols)
     pair = channels // lon_count
     lanes = pair * tile_cols
-    by_pair = increment.reshape(tile_rows, lon_count, lanes).transpose(1, 0, 2)
+    by_pair = increment.reshape(lon_count, pair, tile_rows, tile_cols).transpose(0, 2, 1, 3)
+    by_pair = by_pair.reshape(lon_count, tile_rows, lanes)
     lines_x = lax.all_to_all(by_pair, "lon", 0, 0, tiled=True).reshape(line_x, lanes)
     solved_x = jnp.dot(x_inverse, lines_x, preferred_element_type=jnp.float32).astype(jnp.bfloat16)
     stride = tile_rows // lat_count

time: 146 us -> 154 us (1.055)
  local copies, waits for them, and re-layouts: 10.7 us -> 17.6 us
    reshape x1 -> x2, local copies, waits for them, and re-layouts: 0.08 us -> 3.47 us  [the longest x1 2.67 us: shards(): increment.reshape(lon_count, pair, tile_rows, tile_cols)]
    concatenate x1, local copies, waits for them, and re-layouts: 0.06 us -> 1.61 us  [route_obs(): stacked = jnp.concatenate([innovations, weights, digits], 0)]
    unnamed x13 -> x9, local copies, waits for them, and re-layouts: 2.46 us -> 3.6 us
where the time goes in v6:
time: 154 us; the launch traced here: 153 us
  blocking collectives  91.3 us (59%)
  Pallas kernels  25.4 us (16%)
  local copies, waits for them, and re-layouts  17.6 us (11%)
  matrix products  15.7 us (10%)
  other arithmetic  2.87 us (2%)
    all_to_all x1, blocking collectives, shards(): got = lax.all_to_all(by_row, ('lon', 'lat'), 0, 0, tiled=True)  28.7 us
    pallas_call x1, Pallas kernels, deposit(): pl.pallas_call(deposit_kernel, out_shape=jax.ShapeDtypeStruct((lanes, wid...  25.4 us
    all_to_all x1, blocking collectives, route_obs(): got = lax.all_to_all(send, ('lon', 'lat'), 0, 0, tiled=True)  21.8 us
    all_to_all x1, blocking collectives, shards(): tiles = lax.all_to_all(solved_y, 'lat', 1, 1, tiled=True)  21 us
    all_to_all x1, blocking collectives, shards(): lax.all_to_all(by_pair, 'lon', 0, 0, tiled=True).reshape(line_x, lanes)  19.8 us
    dot_general x1, matrix products, shards(): jnp.dot(x_inverse, lines_x, preferred_element_type=jnp.float32)  7.06 us
    dot_general x1, matrix products, shards(): lax.dot_general(lines_y, y_inverse, (((1,), (1,)), ((), ())), preferred_e...  6.02 us
    unnamed x9, local copies, waits for them, and re-layouts  3.6 us

profile of v6, /device:TPU:0, one launch (start us, length us, event | category | flops | bytes accessed | tf_op | source)
XLA Modules:
  0.0 153.1 jit_solution(13163243101960489117)
XLA Ops:
  0.0 0.9 fusion.9
  0.9 0.1 fusion.17
  1.0 1.2 fusion.4
  2.3 0.7 fusion.16
  3.1 1.6 %concatenate.4 = bf16[23,2048]{1,0:T(8,128)(2,1)S(1)} concatenate(bf16[16,2048]{1,0:T(8,128)(2,1)} %param.9, bf16[4,2048]{1,0:T(4,128)(2,1)} %param.8, bf16[1,2048]{1,0:T(2,128)(2,1)S(1)} %stack.14, bf16[1,2048]{1,0:T(2,128)(2,1)S(1)} %stack.15, bf16[1,2048]{1,0:T(2,128)(2,1)S(1)} %stack.16), dimensions={0} | concatenate | bytes 188416 | tf_op jit(solution)/shard_map/concatenate | solution.py:34
  4.7 0.0 copy-start.2
  4.7 0.4 broadcast_select_fusion
  5.1 0.3 copy-done.2
  5.4 1.2 fusion.7
  6.7 0.5 broadcast.77
  7.2 0.8 reduce.2
  8.0 0.2 copy.58
  8.2 0.3 reshape.164
  8.4 21.8 %all_to_all.24 = bf16[128,2,460]{2,1,0:T(2,128)(2,1)S(1)} all-to-all(bf16[128,2,460]{2,1,0:T(2,128)(2,1)S(1)} %reshape.164), channel_id=1, replica_groups=mesh['lon'=8,'lat'=16] {'lon','lat'}, dimensions={0} | all-to-all | bytes 471040 | tf_op jit(solution)/shard_map/all_to_all | solution.py:42
  30.3 0.4 reshape.165
  30.6 0.7 copy.34
  31.4 0.1 copy.36
  31.5 0.1 reshape.161.by_ref
  31.7 0.1 copy.37
  31.8 0.3 copy.35
  32.1 0.8 slice.28.vals_ref
  32.8 1.7 %copy.38 = bf16[4,128,40]{0,2,1:T(8,128)(2,1)} copy(bf16[4,128,40]{1,2,0:T(8,128)(2,1)S(1)} %slice.39) | data formatting | bytes 81920 | tf_op jit(solution)/shard_map/slice | solution.py:89
  34.5 0.7 add.49.bx_ref
  35.2 0.0 copy-start.1
  35.3 1.3 copy-done.1
  36.6 25.4 %shard_map.64 = bf16[2048,384]{1,0:T(8,128)(2,1)S(1)} custom-call(bf16[16,5120]{1,0:T(8,128)(2,1)S(1)} %slice.28.vals_ref, s32[1,5120]{1,0:T(1,128)S(1)} %reshape.161.by_ref, s32[5120,1]{1,0:T(8,128)S(1)} %add.49.bx_ref, bf16[5120,4]{1,0:T(8,128)(2,1)S(1)} %bitcast.54), custom_call_target="tpu_custom_call" | custom-call | flops 16106127360 | bytes 1818624 | tf_op jit(solution)/shard_map/pallas_call | solution.py:91
  62.0 0.0 copy-start
  62.0 1.1 copy-done
  63.2 2.7 %copy.40 = bf16[8,2,288,128]{3,1,2,0:T(2,128)(2,1)S(1)} copy(bf16[8,2,288,128]{2,3,1,0:T(8,128)(2,1)} %bitcast.53) | data formatting | bytes 2359296 | tf_op jit(solution)/shard_map/reshape | solution.py:132
  65.9 0.8 reshape.153
  66.7 19.8 %all_to_all.25 = bf16[8,288,256]{2,1,0:T(8,128)(2,1)S(1)} all-to-all(bf16[8,288,256]{2,1,0:T(8,128)(2,1)S(1)} %reshape.153), channel_id=1, replica_groups=mesh['lon'=8,'lat'=16] {'lon'}, dimensions={0} | all-to-all | bytes 2359296 | tf_op jit(solution)/shard_map/all_to_all | solution.py:134
  86.4 7.1 %fusion = bf16[2304,256]{0,1:T(8,128)(2,1)S(1)} fusion(bf16[2304,256]{1,0:T(8,128)(2,1)S(1)} %bitcast.61, bf16[2304,2304]{1,0:T(8,128)(2,1)} %param.10), kind=kOutput, calls=%fused_computation.2 | convolution fusion | flops 2718498816 | bytes 12976128 | tf_op jit(solution)/shard_map/dot_general | solution.py:135
  93.5 0.6 copy.41
  94.1 0.1 copy.42
  94.3 0.7 copy.43
  95.0 28.7 %all_to_all.26 = bf16[128,18,256]{2,1,0:T(8,128)(2,1)S(1)} all-to-all(bf16[128,18,256]{2,1,0:T(8,128)(2,1)S(1)} %copy.43), channel_id=1, replica_groups=mesh['lon'=8,'lat'=16] {'lon','lat'}, dimensions={0} | all-to-all | bytes 2359296 | tf_op jit(solution)/shard_map/all_to_all | solution.py:139
  123.7 0.6 reshape.163
  124.2 0.2 copy.45
  124.4 6.0 %fusion.1 = bf16[36,16,8,128]{3,2,1,0:T(8,128)(2,1)S(1)} fusion(bf16[2048,2048]{1,0:T(8,128)(2,1)} %param.11, bf16[36,8,16,128]{3,2,1,0:T(8,128)(2,1)S(1)} %bitcast.62), kind=kOutput, calls=%fused_computation.4 | convolution fusion | flops 2416508928 | bytes 10747904 | tf_op jit(solution)/shard_map/dot_general | solution.py:142
  130.4 0.2 copy.57
  130.6 21.0 %all_to_all.27 = bf16[288,16,128]{2,0,1:T(8,128)(2,1)S(1)} all-to-all(bf16[288,16,128]{2,0,1:T(8,128)(2,1)S(1)} %bitcast.57), channel_id=1, replica_groups=mesh['lon'=8,'lat'=16] {'lat'}, dimensions={1} | all-to-all | bytes 2359296 | tf_op jit(solution)/shard_map/all_to_all | solution.py:146
  151.6 1.5 copy.47
  (9 shorter events, 0.1 us)
Async XLA Ops:
  4.7 0.7 copy-start.2
  35.2 1.3 copy-start.1
  62.0 1.2 copy-start

commit v7 on v1

--- a/solution.py
+++ b/solution.py
@@ -4,13 +4,13 @@
 from jax.sharding import PartitionSpec as P
 
 
-def tile_ranks(owner_tile, groups):
+def tile_ranks(owner_tile, groups, lon_count, lat_count):
     obs_total = owner_tile.shape[0]
     block = 128
     blocks = obs_total // block
-    one_hot = (owner_tile[:, None] == jnp.arange(groups, dtype=jnp.int32)[None, :]).astype(
-        jnp.bfloat16
-    )
+    column = jnp.arange(groups, dtype=jnp.int32)
+    tile_of_column = (column % lon_count) * lat_count + column // lon_count
+    one_hot = (owner_tile[:, None] == tile_of_column[None, :]).astype(jnp.bfloat16)
     hot_blocks = one_hot.reshape(blocks, block, groups)
     inner = jnp.arange(block, dtype=jnp.int32)
     lower = (inner[None, :] <= inner[:, None]).astype(jnp.bfloat16)
@@ -25,7 +25,9 @@
 
 
 def route_obs(owner_tile, corner_cell, weights, innovations, groups, capacity, tile_cols):
-    one_hot, rank = tile_ranks(owner_tile, groups)
+    lon_count = lax.axis_size("lon")
+    lat_count = lax.axis_size("lat")
+    one_hot, rank = tile_ranks(owner_tile, groups, lon_count, lat_count)
     cell_x = corner_cell // (tile_cols - 1)
     cell_y = corner_cell % (tile_cols - 1)
     digits = jnp.stack([cell_y, cell_x % 128, cell_x // 128]).astype(jnp.bfloat16)
@@ -37,7 +39,7 @@
     send = lax.dot_general(
         one_hot, spread, (((0,), (1,)), ((), ())), preferred_element_type=jnp.float32
     ).astype(jnp.bfloat16)
-    got = lax.all_to_all(send, ("lon", "lat"), 0, 0, tiled=True)
+    got = lax.all_to_all(send, ("lat", "lon"), 0, 0, tiled=True)
     got = got.reshape(groups, rows, capacity).transpose(1, 0, 2).reshape(rows, -1)
     return got
 
@@ -91,10 +93,10 @@
     lines_x = lax.all_to_all(by_pair, "lon", 0, 0, tiled=True).reshape(line_x, lanes)
     solved_x = jnp.dot(x_inverse, lines_x, preferred_element_type=jnp.float32).astype(jnp.bfloat16)
     stride = tile_rows // lat_count
-    by_row = solved_x.reshape(lon_count, stride, lat_count, lanes).transpose(0, 2, 1, 3)
+    by_row = solved_x.reshape(lon_count, stride, lat_count, lanes).transpose(2, 0, 1, 3)
     by_row = by_row.reshape(devices, stride, lanes)
-    got = lax.all_to_all(by_row, ("lon", "lat"), 0, 0, tiled=True)
-    got = got.reshape(lon_count, lat_count, stride, pair, tile_cols).transpose(0, 3, 2, 1, 4)
+    got = lax.all_to_all(by_row, ("lat", "lon"), 0, 0, tiled=True)
+    got = got.reshape(lat_count, lon_count, stride, pair, tile_cols).transpose(1, 3, 2, 0, 4)
     lines_y = got.reshape(channels * stride, line_y)
     solved_y = lax.dot_general(
         lines_y, y_inverse, (((1,), (1,)), ((), ())), preferred_element_type=jnp.float32

time: 139 us -> 140 us (level)
  no operation moved by 1% of the time
where the time goes in v7:
time: 140 us
  blocking collectives  91.6 us (65%)
  matrix products  31.8 us (23%)
  local copies, waits for them, and re-layouts  12.5 us (9%)
  other arithmetic  3.71 us (3%)
    all_to_all x1, blocking collectives, shards(): got = lax.all_to_all(by_row, ('lat', 'lon'), 0, 0, tiled=True)  29.2 us
    all_to_all x1, blocking collectives, route_obs(): got = lax.all_to_all(send, ('lat', 'lon'), 0, 0, tiled=True)  21.7 us
    all_to_all x1, blocking collectives, shards(): tiles = lax.all_to_all(solved_y, 'lat', 1, 1, tiled=True)  21 us
    all_to_all x1, blocking collectives, shards(): lax.all_to_all(by_pair, 'lon', 0, 0, tiled=True).reshape(line_x, lanes)  19.8 us
    dot_general x2, matrix products, deposit(): jnp.einsum('cyo,ox->cxy', spread, near_rows, preferred_element_type=jnp.f...  16.2 us
    dot_general x1, matrix products, shards(): jnp.dot(x_inverse, lines_x, preferred_element_type=jnp.float32)  7.06 us
    dot_general x1, matrix products, shards(): lax.dot_general(lines_y, y_inverse, (((1,), (1,)), ((), ())), preferred_e...  6.02 us

profile of v7, /device:TPU:0, one launch (start us, length us, event | category | flops | bytes accessed | tf_op | source)
XLA Modules:
  0.0 139.9 jit_solution(5459620084518930095)
XLA Ops:
  0.0 0.0 copy-start
  0.0 1.0 fusion.48
  1.1 0.1 fusion.58
  1.2 1.2 fusion.41
  2.4 0.7 fusion.57
  3.2 1.6 %concatenate.4 = bf16[23,2048]{1,0:T(8,128)(2,1)S(1)} concatenate(bf16[16,2048]{1,0:T(8,128)(2,1)} %param.9, bf16[4,2048]{1,0:T(4,128)(2,1)} %param.8, bf16[1,2048]{1,0:T(2,128)(2,1)S(1)} %stack.14, bf16[1,2048]{1,0:T(2,128)(2,1)S(1)} %stack.15, bf16[1,2048]{1,0:T(2,128)(2,1)S(1)} %stack.16), dimensions={0} | concatenate | bytes 188416 | tf_op jit(solution)/shard_map/concatenate | solution.py:34
  4.8 0.4 broadcast_select_fusion
  5.2 0.0 copy-done
  5.2 1.3 fusion.46
  6.5 0.5 broadcast.186
  7.0 0.8 reduce.2
  7.8 0.2 copy.52
  8.0 0.3 reshape.245
  8.2 21.7 %all_to_all.24 = bf16[128,2,460]{2,1,0:T(2,128)(2,1)S(1)} all-to-all(bf16[128,2,460]{2,1,0:T(2,128)(2,1)S(1)} %reshape.245), channel_id=1, replica_groups=mesh['lon'=8,'lat'=16] {'lat','lon'}, dimensions={0} | all-to-all | bytes 471040 | tf_op jit(solution)/shard_map/all_to_all | solution.py:42
  29.9 0.4 reshape.246
  30.3 0.7 copy.22
  31.1 0.1 copy.26
  31.2 0.1 reshape.240
  31.3 0.3 iota_compare_fusion.3
  31.6 0.1 copy.23
  31.7 0.1 add.103
  31.9 0.1 copy.24
  32.0 0.1 broadcast_in_dim.117
  32.1 0.1 copy.28
  32.2 0.1 broadcast_in_dim.126
  32.3 0.1 copy.25
  32.5 0.1 broadcast_in_dim.120
  32.6 0.1 copy.29
  32.7 0.1 broadcast_in_dim.128
  32.8 0.3 copy.27
  33.1 0.7 broadcast_in_dim.123
  33.9 0.3 iota_compare_fusion.2
  34.2 7.9 %fusion = f32[288,16,128]{2,0,1:T(8,128)} fusion(pred[128,5120]{1,0:T(8,128)(4,1)S(1)} %iota_compare_fusion.2, bf16[16,5120]{1,0:T(8,128)(2,1)S(1)} %broadcast_in_dim.123, s32[5120]{0:T(1024)S(1)} %broadcast_add_fusion.1, s32[5120]{0:T(1024)S(1)} %add.103, bf16[5120]{0:T(1024)(128)(2,1)S(1)} %broadcast_in_dim.128, bf16[5120]{0:T(1024)(128)(2,1)S(1)} %broadcast_in_dim.126), kind=kOutput, calls=%fused_computation | convolution fusion | flops 6062080000 | bytes 3239936 | tf_op jit(solution)/shard_map/cyo,ox->cxy/dot_general | solution.py:70
  42.1 8.2 %add_convert_fusion = bf16[288,16,128]{2,0,1:T(8,128)(2,1)S(1)} fusion(f32[288,16,128]{2,0,1:T(8,128)} %fusion, pred[128,5120]{1,0:T(8,128)(4,1)S(1)} %iota_compare_fusion.3, bf16[16,5120]{1,0:T(8,128)(2,1)S(1)} %broadcast_in_dim.123, s32[5120]{0:T(1024)S(1)} %broadcast_add_fusion.1, s32[5120]{0:T(1024)S(1)} %add.103, ...), kind=kOutput, calls=%fused_computation.30 | convolution fusion | flops 6063259648 | bytes 4419584 | tf_op jit(solution)/shard_map/cyo,ox->cxy/dot_general | solution.py:70
  50.4 1.0 copy.51
  51.4 0.8 reshape.232
  52.2 19.8 %all_to_all.25 = bf16[8,288,256]{2,1,0:T(8,128)(2,1)S(1)} all-to-all(bf16[8,288,256]{2,1,0:T(8,128)(2,1)S(1)} %reshape.232), channel_id=1, replica_groups=mesh['lon'=8,'lat'=16] {'lon'}, dimensions={0} | all-to-all | bytes 2359296 | tf_op jit(solution)/shard_map/all_to_all | solution.py:93
  72.0 7.1 %fusion.14 = bf16[2304,256]{0,1:T(8,128)(2,1)S(1)} fusion(bf16[2304,256]{1,0:T(8,128)(2,1)S(1)} %bitcast.66, bf16[2304,2304]{1,0:T(8,128)(2,1)} %param.10), kind=kOutput, calls=%fused_computation.18 | convolution fusion | flops 2718498816 | bytes 12976128 | tf_op jit(solution)/shard_map/dot_general | solution.py:94
  79.0 0.6 copy.31
  79.6 0.7 copy.50
  80.3 0.7 copy.33
  81.0 29.2 %all_to_all.26 = bf16[128,18,256]{2,1,0:T(8,128)(2,1)S(1)} all-to-all(bf16[128,18,256]{2,1,0:T(8,128)(2,1)S(1)} %copy.33), channel_id=1, replica_groups=mesh['lon'=8,'lat'=16] {'lat','lon'}, dimensions={0} | all-to-all | bytes 2359296 | tf_op jit(solution)/shard_map/all_to_all | solution.py:98
  110.2 0.6 reshape.244
  110.7 0.5 copy.35
  111.2 6.0 %fusion.37 = bf16[36,16,8,128]{3,2,1,0:T(8,128)(2,1)S(1)} fusion(bf16[2048,2048]{1,0:T(8,128)(2,1)} %param.11, bf16[36,8,16,128]{3,2,1,0:T(8,128)(2,1)S(1)} %bitcast.67), kind=kOutput, calls=%fused_computation.37 | convolution fusion | flops 2416508928 | bytes 10747904 | tf_op jit(solution)/shard_map/dot_general | solution.py:101
  117.2 0.2 copy.49
  117.5 21.0 %all_to_all.27 = bf16[288,16,128]{2,0,1:T(8,128)(2,1)S(1)} all-to-all(bf16[288,16,128]{2,0,1:T(8,128)(2,1)S(1)} %bitcast.62), channel_id=1, replica_groups=mesh['lon'=8,'lat'=16] {'lat'}, dimensions={1} | all-to-all | bytes 2359296 | tf_op jit(solution)/shard_map/all_to_all | solution.py:105
  138.5 1.5 %copy.37 = bf16[288,16,128]{2,1,0:T(8,128)(2,1)} copy(bf16[288,16,128]{2,0,1:T(8,128)(2,1)S(1)} %all_to_all.27) | data formatting | bytes 2359296 | tf_op jit(solution)/shard_map/all_to_all | solution.py:105
  (11 shorter events, 0.1 us)
Async XLA Ops:
  0.0 5.2 %copy-start = (s32[2048]{0:T(1024)S(1)}, s32[2048]{0:T(1024)}, u32[]{:S(2)}) copy-start(s32[2048]{0:T(1024)} %param.6) | copy-start | bytes 24580

commit v8 on v1

--- a/solution.py
+++ b/solution.py
@@ -91,8 +91,8 @@
     lines_x = lax.all_to_all(by_pair, "lon", 0, 0, tiled=True).reshape(line_x, lanes)
     solved_x = jnp.dot(x_inverse, lines_x, preferred_element_type=jnp.float32).astype(jnp.bfloat16)
     stride = tile_rows // lat_count
-    by_row = solved_x.reshape(lon_count, stride, lat_count, lanes).transpose(0, 2, 1, 3)
-    by_row = by_row.reshape(devices, stride, lanes)
+    by_row = solved_x.reshape(lon_count, stride, lat_count, pair, tile_cols).transpose(0, 2, 1, 3, 4)
+    by_row = by_row.reshape(devices, stride * pair, tile_cols)
     got = lax.all_to_all(by_row, ("lon", "lat"), 0, 0, tiled=True)
     got = got.reshape(lon_count, lat_count, stride, pair, tile_cols).transpose(0, 3, 2, 1, 4)
     lines_y = got.reshape(channels * stride, line_y)

time: 139 us -> 137 us (0.986)
  blocking collectives: 91.3 us -> 88.6 us
    all_to_all x1, blocking collectives: 28.7 us -> 25.9 us  [shards(): got = lax.all_to_all(by_row, ('lon', 'lat'), 0, 0, tiled=True)]
where the time goes in v8:
time: 137 us; the launch traced here: 136 us
  blocking collectives  88.6 us (65%)
  matrix products  31.8 us (23%)
  local copies, waits for them, and re-layouts  12 us (9%)
  other arithmetic  3.65 us (3%)
    all_to_all x1, blocking collectives, shards(): got = lax.all_to_all(by_row, ('lon', 'lat'), 0, 0, tiled=True)  25.9 us
    all_to_all x1, blocking collectives, route_obs(): got = lax.all_to_all(send, ('lon', 'lat'), 0, 0, tiled=True)  21.8 us
    all_to_all x1, blocking collectives, shards(): tiles = lax.all_to_all(solved_y, 'lat', 1, 1, tiled=True)  21.1 us
    all_to_all x1, blocking collectives, shards(): lax.all_to_all(by_pair, 'lon', 0, 0, tiled=True).reshape(line_x, lanes)  19.8 us
    dot_general x2, matrix products, deposit(): jnp.einsum('cyo,ox->cxy', spread, near_rows, preferred_element_type=jnp.f...  16.2 us
    dot_general x1, matrix products, shards(): jnp.dot(x_inverse, lines_x, preferred_element_type=jnp.float32)  7.06 us
    dot_general x1, matrix products, shards(): lax.dot_general(lines_y, y_inverse, (((1,), (1,)), ((), ())), preferred_e...  6.02 us

profile of v8, /device:TPU:0, one launch (start us, length us, event | category | flops | bytes accessed | tf_op | source)
XLA Modules:
  0.0 136.3 jit_solution(14390288255480441868)
XLA Ops:
  0.0 1.0 fusion.45
  1.0 0.1 fusion.53
  1.1 1.2 fusion.40
  2.3 0.7 fusion.52
  3.2 1.6 %concatenate.4 = bf16[23,2048]{1,0:T(8,128)(2,1)S(1)} concatenate(bf16[16,2048]{1,0:T(8,128)(2,1)} %param.9, bf16[4,2048]{1,0:T(4,128)(2,1)} %param.8, bf16[1,2048]{1,0:T(2,128)(2,1)S(1)} %stack.14, bf16[1,2048]{1,0:T(2,128)(2,1)S(1)} %stack.15, bf16[1,2048]{1,0:T(2,128)(2,1)S(1)} %stack.16), dimensions={0} | concatenate | bytes 188416 | tf_op jit(solution)/shard_map/concatenate | solution.py:32
  4.8 0.4 broadcast_select_fusion
  5.1 0.0 copy-done
  5.2 1.3 fusion.43
  6.4 0.5 broadcast.125
  6.9 0.8 reduce.2
  7.7 0.2 copy.48
  7.9 0.3 reshape.216
  8.2 21.8 %all_to_all.24 = bf16[128,2,460]{2,1,0:T(2,128)(2,1)S(1)} all-to-all(bf16[128,2,460]{2,1,0:T(2,128)(2,1)S(1)} %reshape.216), channel_id=1, replica_groups=mesh['lon'=8,'lat'=16] {'lon','lat'}, dimensions={0} | all-to-all | bytes 471040 | tf_op jit(solution)/shard_map/all_to_all | solution.py:40
  30.0 0.4 reshape.217
  30.4 0.7 copy.22
  31.2 0.1 copy.26
  31.3 0.1 reshape.212
  31.4 0.3 iota_compare_fusion.3
  31.7 0.1 copy.23
  31.8 0.1 add.75
  32.0 0.1 copy.24
  32.1 0.1 broadcast_in_dim.117
  32.2 0.1 copy.28
  32.3 0.1 broadcast_in_dim.126
  32.4 0.1 copy.25
  32.6 0.1 broadcast_in_dim.120
  32.7 0.1 copy.29
  32.8 0.1 broadcast_in_dim.128
  32.9 0.3 copy.27
  33.2 0.7 broadcast_in_dim.123
  33.9 0.3 iota_compare_fusion.2
  34.3 7.9 %fusion = f32[288,16,128]{2,0,1:T(8,128)} fusion(pred[128,5120]{1,0:T(8,128)(4,1)S(1)} %iota_compare_fusion.2, bf16[16,5120]{1,0:T(8,128)(2,1)S(1)} %broadcast_in_dim.123, s32[5120]{0:T(1024)S(1)} %broadcast_add_fusion.1, s32[5120]{0:T(1024)S(1)} %add.75, bf16[5120]{0:T(1024)(128)(2,1)S(1)} %broadcast_in_dim.128, bf16[5120]{0:T(1024)(128)(2,1)S(1)} %broadcast_in_dim.126), kind=kOutput, calls=%fused_computation | convolution fusion | flops 6062080000 | bytes 3239936 | tf_op jit(solution)/shard_map/cyo,ox->cxy/dot_general | solution.py:68
  42.2 8.2 %add_convert_fusion = bf16[288,16,128]{2,0,1:T(8,128)(2,1)S(1)} fusion(f32[288,16,128]{2,0,1:T(8,128)} %fusion, pred[128,5120]{1,0:T(8,128)(4,1)S(1)} %iota_compare_fusion.3, bf16[16,5120]{1,0:T(8,128)(2,1)S(1)} %broadcast_in_dim.123, s32[5120]{0:T(1024)S(1)} %broadcast_add_fusion.1, s32[5120]{0:T(1024)S(1)} %add.75, ...), kind=kOutput, calls=%fused_computation.30 | convolution fusion | flops 6063259648 | bytes 4419584 | tf_op jit(solution)/shard_map/cyo,ox->cxy/dot_general | solution.py:68
  50.5 1.0 copy.47
  51.5 0.8 reshape.204
  52.3 19.8 %all_to_all.25 = bf16[8,288,256]{2,1,0:T(8,128)(2,1)S(1)} all-to-all(bf16[8,288,256]{2,1,0:T(8,128)(2,1)S(1)} %reshape.204), channel_id=1, replica_groups=mesh['lon'=8,'lat'=16] {'lon'}, dimensions={0} | all-to-all | bytes 2359296 | tf_op jit(solution)/shard_map/all_to_all | solution.py:91
  72.0 7.1 %fusion.14 = bf16[2304,256]{0,1:T(8,128)(2,1)S(1)} fusion(bf16[2304,256]{1,0:T(8,128)(2,1)S(1)} %bitcast.63, bf16[2304,2304]{1,0:T(8,128)(2,1)} %param.10), kind=kOutput, calls=%fused_computation.18 | convolution fusion | flops 2718498816 | bytes 12976128 | tf_op jit(solution)/shard_map/dot_general | solution.py:92
  79.1 0.6 copy.31
  79.7 0.3 reshape.206
  80.1 0.3 copy.32
  80.3 0.8 copy.33
  81.1 25.9 %all_to_all.26 = bf16[128,36,128]{2,1,0:T(8,128)(2,1)S(1)} all-to-all(bf16[128,36,128]{2,1,0:T(8,128)(2,1)S(1)} %copy.33), channel_id=1, replica_groups=mesh['lon'=8,'lat'=16] {'lon','lat'}, dimensions={0} | all-to-all | bytes 2359296 | tf_op jit(solution)/shard_map/all_to_all | solution.py:96
  107.1 0.3 copy.34
  107.3 0.2 copy.35
  107.6 6.0 %fusion.37 = bf16[36,16,8,128]{3,2,1,0:T(8,128)(2,1)S(1)} fusion(bf16[2048,2048]{1,0:T(8,128)(2,1)} %param.11, bf16[36,8,16,128]{3,2,1,0:T(8,128)(2,1)S(1)} %bitcast.64), kind=kOutput, calls=%fused_computation.37 | convolution fusion | flops 2416508928 | bytes 10747904 | tf_op jit(solution)/shard_map/dot_general | solution.py:99
  113.6 0.2 copy.46
  113.8 21.1 %all_to_all.27 = bf16[288,16,128]{2,0,1:T(8,128)(2,1)S(1)} all-to-all(bf16[288,16,128]{2,0,1:T(8,128)(2,1)S(1)} %bitcast.61), channel_id=1, replica_groups=mesh['lon'=8,'lat'=16] {'lat'}, dimensions={1} | all-to-all | bytes 2359296 | tf_op jit(solution)/shard_map/all_to_all | solution.py:103
  134.9 1.5 %copy.37 = bf16[288,16,128]{2,1,0:T(8,128)(2,1)} copy(bf16[288,16,128]{2,0,1:T(8,128)(2,1)S(1)} %all_to_all.27) | data formatting | bytes 2359296 | tf_op jit(solution)/shard_map/all_to_all | solution.py:103
  (11 shorter events, 0.1 us)
Async XLA Ops:
  0.0 5.1 %copy-start = (s32[2048]{0:T(1024)S(1)}, s32[2048]{0:T(1024)}, u32[]{:S(2)}) copy-start(s32[2048]{0:T(1024)} %param.6) | copy-start | bytes 24580

commit v9 on v8

--- a/solution.py
+++ b/solution.py
@@ -37,7 +37,10 @@
     send = lax.dot_general(
         one_hot, spread, (((0,), (1,)), ((), ())), preferred_element_type=jnp.float32
     ).astype(jnp.bfloat16)
-    got = lax.all_to_all(send, ("lon", "lat"), 0, 0, tiled=True)
+    message = send.shape[1]
+    padded = -(-message // 1024) * 1024
+    send = jnp.pad(send, ((0, 0), (0, padded - message)))
+    got = lax.all_to_all(send, ("lon", "lat"), 0, 0, tiled=True)[:, :message]
     got = got.reshape(groups, rows, capacity).transpose(1, 0, 2).reshape(rows, -1)
     return got
 

time: 137 us -> 136 us (level)
  no operation moved by 1% of the time
where the time goes in v9:
time: 136 us
  blocking collectives  88.6 us (65%)
  matrix products  31.8 us (23%)
  local copies, waits for them, and re-layouts  11.2 us (8%)
  other arithmetic  3.66 us (3%)
    all_to_all x1, blocking collectives, shards(): got = lax.all_to_all(by_row, ('lon', 'lat'), 0, 0, tiled=True)  25.9 us
    all_to_all x1, blocking collectives, route_obs(): got = lax.all_to_all(send, ('lon', 'lat'), 0, 0, tiled=True)[:, :message]  21.8 us
    all_to_all x1, blocking collectives, shards(): tiles = lax.all_to_all(solved_y, 'lat', 1, 1, tiled=True)  21.1 us
    all_to_all x1, blocking collectives, shards(): lax.all_to_all(by_pair, 'lon', 0, 0, tiled=True).reshape(line_x, lanes)  19.8 us
    dot_general x2, matrix products, deposit(): jnp.einsum('cyo,ox->cxy', spread, near_rows, preferred_element_type=jnp.f...  16.2 us
    dot_general x1, matrix products, shards(): jnp.dot(x_inverse, lines_x, preferred_element_type=jnp.float32)  7.06 us
    dot_general x1, matrix products, shards(): lax.dot_general(lines_y, y_inverse, (((1,), (1,)), ((), ())), preferred_e...  6.02 us

profile of v9, /device:TPU:0, one launch (start us, length us, event | category | flops | bytes accessed | tf_op | source)
XLA Modules:
  0.0 135.6 jit_solution(7925375540071086710)
XLA Ops:
  0.0 1.0 fusion.44
  1.0 0.1 fusion.52
  1.1 1.2 fusion.40
  2.3 0.7 fusion.51
  3.2 1.6 %concatenate.4 = bf16[23,2048]{1,0:T(8,128)(2,1)S(1)} concatenate(bf16[16,2048]{1,0:T(8,128)(2,1)} %param.9, bf16[4,2048]{1,0:T(4,128)(2,1)} %param.8, bf16[1,2048]{1,0:T(2,128)(2,1)S(1)} %stack.14, bf16[1,2048]{1,0:T(2,128)(2,1)S(1)} %stack.15, bf16[1,2048]{1,0:T(2,128)(2,1)S(1)} %stack.16), dimensions={0} | concatenate | bytes 188416 | tf_op jit(solution)/shard_map/concatenate | solution.py:32
  4.8 0.4 broadcast_select_fusion
  5.2 1.3 convolution_convert_fusion.2
  6.4 0.5 broadcast.127
  6.9 0.8 reduce.2
  7.8 0.1 copy.51
  7.9 0.2 reshape.215
  8.1 21.8 %all_to_all.27 = bf16[128,2,512]{2,1,0:T(2,128)(2,1)S(1)} all-to-all(bf16[128,2,512]{2,1,0:T(2,128)(2,1)S(1)} %reshape.215), channel_id=1, replica_groups=mesh['lon'=8,'lat'=16] {'lon','lat'}, dimensions={0} | all-to-all | bytes 524288 | tf_op jit(solution)/shard_map/all_to_all | solution.py:43
  29.9 0.2 reshape.216
  30.2 0.1 copy.50
  30.3 0.2 copy.22
  30.5 0.1 copy.26
  30.6 0.1 reshape.211
  30.7 0.3 iota_compare_fusion.3
  31.0 0.1 copy.23
  31.1 0.1 add.77
  31.3 0.1 copy.24
  31.4 0.1 broadcast_in_dim.117
  31.5 0.1 copy.28
  31.6 0.1 broadcast_in_dim.126
  31.7 0.1 copy.25
  31.9 0.1 broadcast_in_dim.120
  32.0 0.1 copy.29
  32.1 0.1 broadcast_in_dim.128
  32.2 0.3 copy.27
  32.5 0.7 broadcast_in_dim.123
  33.3 0.3 iota_compare_fusion.2
  33.6 7.9 %fusion = f32[288,16,128]{2,0,1:T(8,128)} fusion(pred[128,5120]{1,0:T(8,128)(4,1)S(1)} %iota_compare_fusion.2, bf16[16,5120]{1,0:T(8,128)(2,1)S(1)} %broadcast_in_dim.123, s32[5120]{0:T(1024)S(1)} %broadcast_add_fusion.1, s32[5120]{0:T(1024)S(1)} %add.77, bf16[5120]{0:T(1024)(128)(2,1)S(1)} %broadcast_in_dim.128, bf16[5120]{0:T(1024)(128)(2,1)S(1)} %broadcast_in_dim.126), kind=kOutput, calls=%fused_computation | convolution fusion | flops 6062080000 | bytes 3239936 | tf_op jit(solution)/shard_map/cyo,ox->cxy/dot_general | solution.py:71
  41.5 8.2 %add_convert_fusion = bf16[288,16,128]{2,0,1:T(8,128)(2,1)S(1)} fusion(f32[288,16,128]{2,0,1:T(8,128)} %fusion, pred[128,5120]{1,0:T(8,128)(4,1)S(1)} %iota_compare_fusion.3, bf16[16,5120]{1,0:T(8,128)(2,1)S(1)} %broadcast_in_dim.123, s32[5120]{0:T(1024)S(1)} %broadcast_add_fusion.1, s32[5120]{0:T(1024)S(1)} %add.77, ...), kind=kOutput, calls=%fused_computation.30 | convolution fusion | flops 6063259648 | bytes 4419584 | tf_op jit(solution)/shard_map/cyo,ox->cxy/dot_general | solution.py:71
  49.8 1.0 copy.49
  50.8 0.8 reshape.203
  51.6 19.8 %all_to_all.28 = bf16[8,288,256]{2,1,0:T(8,128)(2,1)S(1)} all-to-all(bf16[8,288,256]{2,1,0:T(8,128)(2,1)S(1)} %reshape.203), channel_id=1, replica_groups=mesh['lon'=8,'lat'=16] {'lon'}, dimensions={0} | all-to-all | bytes 2359296 | tf_op jit(solution)/shard_map/all_to_all | solution.py:94
  71.3 7.1 %fusion.14 = bf16[2304,256]{0,1:T(8,128)(2,1)S(1)} fusion(bf16[2304,256]{1,0:T(8,128)(2,1)S(1)} %bitcast.67, bf16[2304,2304]{1,0:T(8,128)(2,1)} %param.10), kind=kOutput, calls=%fused_computation.18 | convolution fusion | flops 2718498816 | bytes 12976128 | tf_op jit(solution)/shard_map/dot_general | solution.py:95
  78.4 0.6 copy.31
  79.0 0.3 reshape.205
  79.4 0.3 copy.32
  79.6 0.8 copy.33
  80.4 25.9 %all_to_all.29 = bf16[128,36,128]{2,1,0:T(8,128)(2,1)S(1)} all-to-all(bf16[128,36,128]{2,1,0:T(8,128)(2,1)S(1)} %copy.33), channel_id=1, replica_groups=mesh['lon'=8,'lat'=16] {'lon','lat'}, dimensions={0} | all-to-all | bytes 2359296 | tf_op jit(solution)/shard_map/all_to_all | solution.py:99
  106.4 0.3 copy.34
  106.6 0.2 copy.35
  106.9 6.0 %fusion.37 = bf16[36,16,8,128]{3,2,1,0:T(8,128)(2,1)S(1)} fusion(bf16[2048,2048]{1,0:T(8,128)(2,1)} %param.11, bf16[36,8,16,128]{3,2,1,0:T(8,128)(2,1)S(1)} %bitcast.68), kind=kOutput, calls=%fused_computation.37 | convolution fusion | flops 2416508928 | bytes 10747904 | tf_op jit(solution)/shard_map/dot_general | solution.py:102
  112.9 0.2 copy.48
  113.1 21.1 %all_to_all.30 = bf16[288,16,128]{2,0,1:T(8,128)(2,1)S(1)} all-to-all(bf16[288,16,128]{2,0,1:T(8,128)(2,1)S(1)} %bitcast.65), channel_id=1, replica_groups=mesh['lon'=8,'lat'=16] {'lat'}, dimensions={1} | all-to-all | bytes 2359296 | tf_op jit(solution)/shard_map/all_to_all | solution.py:106
  134.2 1.5 %copy.37 = bf16[288,16,128]{2,1,0:T(8,128)(2,1)} copy(bf16[288,16,128]{2,0,1:T(8,128)(2,1)S(1)} %all_to_all.30) | data formatting | bytes 2359296 | tf_op jit(solution)/shard_map/all_to_all | solution.py:106
  (13 shorter events, 0.1 us)
Async XLA Ops:
  0.0 5.1 %copy-start = (s32[2048]{0:T(1024)S(1)}, s32[2048]{0:T(1024)}, u32[]{:S(2)}) copy-start(s32[2048]{0:T(1024)} %param.6) | copy-start | bytes 24580

commit v10 on v8

--- a/solution.py
+++ b/solution.py
@@ -50,7 +50,7 @@
     row_iota = jnp.arange(tile_rows, dtype=jnp.int32)
     col_iota = jnp.arange(tile_cols, dtype=jnp.int32)
     zero_value = jnp.zeros((), jnp.bfloat16)
-    raw_total = jnp.zeros((channels, tile_rows, tile_cols), jnp.float32)
+    raw_total = None
     for offset_y in range(2):
         near_rows = jnp.where(
             row_iota[None, :] == base_x[:, None], got_weights[2 * offset_y][:, None], zero_value
@@ -65,9 +65,8 @@
             values[:, None, :],
             zero_value,
         )
-        raw_total = raw_total + jnp.einsum(
-            "cyo,ox->cxy", spread, near_rows, preferred_element_type=jnp.float32
-        )
+        part = jnp.einsum("cyo,ox->cxy", spread, near_rows, preferred_element_type=jnp.float32)
+        raw_total = part.astype(jnp.bfloat16) if raw_total is None else part + raw_total
     return raw_total.astype(jnp.bfloat16)
 
 

time: 137 us -> 134 us (0.978)
  matrix products: 31.8 us -> 29.3 us
    dot_general x2, matrix products: 16.2 us -> 13.6 us  [deposit(): jnp.einsum('cyo,ox->cxy', spread, near_rows, preferred_element_type=jnp.f...]
where the time goes in v10:
time: 134 us
  blocking collectives  88.6 us (66%)
  matrix products  29.3 us (22%)
  local copies, waits for them, and re-layouts  12 us (9%)
  other arithmetic  3.59 us (3%)
    all_to_all x1, blocking collectives, shards(): got = lax.all_to_all(by_row, ('lon', 'lat'), 0, 0, tiled=True)  25.9 us
    all_to_all x1, blocking collectives, route_obs(): got = lax.all_to_all(send, ('lon', 'lat'), 0, 0, tiled=True)  21.8 us
    all_to_all x1, blocking collectives, shards(): tiles = lax.all_to_all(solved_y, 'lat', 1, 1, tiled=True)  21.1 us
    all_to_all x1, blocking collectives, shards(): lax.all_to_all(by_pair, 'lon', 0, 0, tiled=True).reshape(line_x, lanes)  19.8 us
    dot_general x2, matrix products, deposit(): jnp.einsum('cyo,ox->cxy', spread, near_rows, preferred_element_type=jnp.f...  13.6 us
    dot_general x1, matrix products, shards(): jnp.dot(x_inverse, lines_x, preferred_element_type=jnp.float32)  7.06 us
    dot_general x1, matrix products, shards(): lax.dot_general(lines_y, y_inverse, (((1,), (1,)), ((), ())), preferred_e...  6.02 us

profile of v10, /device:TPU:0, one launch (start us, length us, event | category | flops | bytes accessed | tf_op | source)
XLA Modules:
  0.0 133.8 jit_solution(16434671878709773308)
XLA Ops:
  0.0 0.7 fusion.57
  0.8 0.9 fusion.50
  1.7 0.1 fusion.58
  1.8 1.2 fusion.45
  3.1 1.6 %concatenate.4 = bf16[23,2048]{1,0:T(8,128)(2,1)S(1)} concatenate(bf16[16,2048]{1,0:T(8,128)(2,1)} %param.9, bf16[4,2048]{1,0:T(4,128)(2,1)} %param.8, bf16[1,2048]{1,0:T(2,128)(2,1)S(1)} %stack.14, bf16[1,2048]{1,0:T(2,128)(2,1)S(1)} %stack.15, bf16[1,2048]{1,0:T(2,128)(2,1)S(1)} %stack.16), dimensions={0} | concatenate | bytes 188416 | tf_op jit(solution)/shard_map/concatenate | solution.py:32
  4.7 0.4 broadcast_select_fusion
  5.1 0.0 copy-done
  5.1 1.3 fusion.48
  6.3 0.5 broadcast.125
  6.9 0.8 reduce.2
  7.7 0.2 copy.48
  7.8 0.3 reshape.216
  8.1 21.8 %all_to_all.24 = bf16[128,2,460]{2,1,0:T(2,128)(2,1)S(1)} all-to-all(bf16[128,2,460]{2,1,0:T(2,128)(2,1)S(1)} %reshape.216), channel_id=1, replica_groups=mesh['lon'=8,'lat'=16] {'lon','lat'}, dimensions={0} | all-to-all | bytes 471040 | tf_op jit(solution)/shard_map/all_to_all | solution.py:40
  29.9 0.4 reshape.217
  30.3 0.7 copy.22
  31.1 0.1 copy.26
  31.2 0.1 reshape.212
  31.3 0.3 iota_compare_fusion.2
  31.7 0.1 copy.28
  31.8 0.1 broadcast_in_dim.126
  31.9 0.1 copy.29
  32.0 0.1 broadcast_in_dim.128
  32.2 0.1 copy.23
  32.3 0.1 add.75
  32.4 0.3 copy.27
  32.7 0.7 broadcast_in_dim.123
  33.4 0.3 iota_compare_fusion.3
  33.8 0.1 copy.24
  33.9 0.1 broadcast_in_dim.117
  34.0 0.1 copy.25
  34.1 0.1 broadcast_in_dim.120
  34.2 6.5 %fusion.31 = bf16[288,16,128]{2,0,1:T(8,128)(2,1)S(1)} fusion(pred[128,5120]{1,0:T(8,128)(4,1)S(1)} %iota_compare_fusion.2, bf16[16,5120]{1,0:T(8,128)(2,1)S(1)} %broadcast_in_dim.123, s32[5120]{0:T(1024)S(1)} %broadcast_add_fusion.1, s32[5120]{0:T(1024)S(1)} %add.75, bf16[5120]{0:T(1024)(128)(2,1)S(1)} %broadcast_in_dim.128, ...), kind=kOutput, calls=%fused_computation.31 | convolution fusion | flops 6062669824 | bytes 2060288 | tf_op jit(solution)/shard_map/cyo,ox->cxy/dot_general | solution.py:68
  40.8 7.1 %add_convert_fusion = bf16[288,16,128]{2,0,1:T(8,128)(2,1)S(1)} fusion(bf16[288,16,128]{2,0,1:T(8,128)(2,1)S(1)} %fusion.31, pred[128,5120]{1,0:T(8,128)(4,1)S(1)} %iota_compare_fusion.3, bf16[16,5120]{1,0:T(8,128)(2,1)S(1)} %broadcast_in_dim.123, s32[5120]{0:T(1024)S(1)} %broadcast_add_fusion.1, s32[5120]{0:T(1024)S(1)} %add.75, ...), kind=kOutput, calls=%fused_computation.30 | convolution fusion | flops 6063849472 | bytes 3239936 | tf_op jit(solution)/shard_map/cyo,ox->cxy/dot_general | solution.py:68
  47.9 1.0 copy.47
  48.9 0.8 reshape.204
  49.7 19.8 %all_to_all.25 = bf16[8,288,256]{2,1,0:T(8,128)(2,1)S(1)} all-to-all(bf16[8,288,256]{2,1,0:T(8,128)(2,1)S(1)} %reshape.204), channel_id=1, replica_groups=mesh['lon'=8,'lat'=16] {'lon'}, dimensions={0} | all-to-all | bytes 2359296 | tf_op jit(solution)/shard_map/all_to_all | solution.py:90
  69.5 7.1 %fusion.14 = bf16[2304,256]{0,1:T(8,128)(2,1)S(1)} fusion(bf16[2304,256]{1,0:T(8,128)(2,1)S(1)} %bitcast.65, bf16[2304,2304]{1,0:T(8,128)(2,1)} %param.10), kind=kOutput, calls=%fused_computation.18 | convolution fusion | flops 2718498816 | bytes 12976128 | tf_op jit(solution)/shard_map/dot_general | solution.py:91
  76.5 0.6 copy.31
  77.2 0.3 reshape.206
  77.5 0.3 copy.32
  77.8 0.8 copy.33
  78.5 25.9 %all_to_all.26 = bf16[128,36,128]{2,1,0:T(8,128)(2,1)S(1)} all-to-all(bf16[128,36,128]{2,1,0:T(8,128)(2,1)S(1)} %copy.33), channel_id=1, replica_groups=mesh['lon'=8,'lat'=16] {'lon','lat'}, dimensions={0} | all-to-all | bytes 2359296 | tf_op jit(solution)/shard_map/all_to_all | solution.py:95
  104.5 0.3 copy.34
  104.8 0.2 copy.35
  105.0 6.0 %fusion.42 = bf16[36,16,8,128]{3,2,1,0:T(8,128)(2,1)S(1)} fusion(bf16[2048,2048]{1,0:T(8,128)(2,1)} %param.11, bf16[36,8,16,128]{3,2,1,0:T(8,128)(2,1)S(1)} %bitcast.66), kind=kOutput, calls=%fused_computation.38 | convolution fusion | flops 2416508928 | bytes 10747904 | tf_op jit(solution)/shard_map/dot_general | solution.py:98
  111.0 0.2 copy.46
  111.2 21.1 %all_to_all.27 = bf16[288,16,128]{2,0,1:T(8,128)(2,1)S(1)} all-to-all(bf16[288,16,128]{2,0,1:T(8,128)(2,1)S(1)} %bitcast.63), channel_id=1, replica_groups=mesh['lon'=8,'lat'=16] {'lat'}, dimensions={1} | all-to-all | bytes 2359296 | tf_op jit(solution)/shard_map/all_to_all | solution.py:102
  132.3 1.5 %copy.37 = bf16[288,16,128]{2,1,0:T(8,128)(2,1)} copy(bf16[288,16,128]{2,0,1:T(8,128)(2,1)S(1)} %all_to_all.27) | data formatting | bytes 2359296 | tf_op jit(solution)/shard_map/all_to_all | solution.py:102
  (11 shorter events, 0.1 us)
Async XLA Ops:
  0.0 5.1 %copy-start = (s32[2048]{0:T(1024)S(1)}, s32[2048]{0:T(1024)}, u32[]{:S(2)}) copy-start(s32[2048]{0:T(1024)} %param.6) | copy-start | bytes 24580
